TPU v7x, 256 devices: a whole 4x4x8 slice. The times are simulated.
256 devices in a mesh: aux: 16 (over z_hi, y, core), virt: 16 (over x, z_lo).
Axes of the slice: x: 4, y: 4, z: 8 (z_hi: 2, z_lo: 4; z = z_hi * 4 + z_lo), core: 2. Of those that a mesh axis runs over, the one named last changes fastest.
Arguments:
- row_codes: bfloat16 [16, 128, 1920], P('aux'), may hold values from -4 to 4
- row_scales: float32 [16, 128, 15], P('aux'), may hold values from 0.2 to 2
- panel_codes: bfloat16 [16, 1920, 1920], P('aux', 'virt'), may hold values from -4 to 4
- panel_scales: float32 [16, 1920, 15], P('aux', 'virt'), may hold values from 0.0017116329 to 0.01711633
- amplitudes: bfloat16 [64, 1920, 1920], P('aux', 'virt'), may hold values from -0.125 to 0.125
Outputs:
- residual: float32 [1920, 64, 128], P('virt', 'aux')
All inputs are finite; a program needn't handle non-finite values.
Results may differ from a plain program's by a relative error of at most 0.005.
Values may be sent and summed in bfloat16 or wider, within the bound.
No kernel may reach another device: no remote copies, remote signals or barrier semaphores. Data moves between devices by JAX's collectives and lax.ppermute only.
A program may use at most 128 MiB of HBM per device.

v0:
```python
import jax
import jax.numpy as jnp
from jax import lax
from jax.sharding import PartitionSpec as P


def decode_rows(codes, scales):
    count, width, length = codes.shape
    blocks = scales.shape[2]
    wide = (
        codes.astype(jnp.float32).reshape(count, width, blocks, length // blocks)
        * scales[:, :, :, None]
    )
    return wide.reshape(count, width, length).astype(jnp.bfloat16)


def on_device(row_codes, row_scales, panel_codes, panel_scales, amplitudes):
    row_local = decode_rows(row_codes, row_scales)
    panel_local = decode_rows(panel_codes, panel_scales)
    row_all = lax.all_gather(row_local, "aux", axis=0, tiled=True)
    half = jnp.einsum(
        "qac,pdc->pqda", row_all, amplitudes, preferred_element_type=jnp.float32
    ).astype(jnp.bfloat16)
    total = jnp.einsum(
        "qdb,pqda->bpa",
        lax.all_gather(panel_local, "aux", axis=0, tiled=True),
        half,
        preferred_element_type=jnp.float32,
    )
    return lax.psum_scatter(total, "virt", scatter_dimension=0, tiled=True)


def solution(mesh):
    placed = (
        P("aux", None, None),
        P("aux", None, None),
        P("aux", "virt", None),
        P("aux", "virt", None),
        P("aux", "virt", None),
    )
    return jax.shard_map(
        on_device, mesh=mesh, in_specs=placed, out_specs=P("virt", "aux", None), check_vma=False
    )
```

profile of v0, /device:TPU:8, one launch (start us, length us, event | category | flops | bytes accessed | tf_op | source)
XLA Modules:
  0.0 329.5 jit_solution(167404000206299236)
XLA Ops:
  6.5 0.0 copy-start
  6.5 0.0 copy-start.1
  6.5 0.0 all-gather.5.cloned.1.call-start
  6.5 0.8 copy.21
  7.4 1.3 copy.13
  8.7 0.1 fusion.10
  8.8 1.0 copy.14
  9.8 0.0 all-gather.5.cloned.1.call-update
  9.8 0.0 all-gather.3.cloned.1.call-start
  9.9 0.8 copy.18
  10.7 0.3 mul.33
  11.0 1.2 mul.34
  12.2 0.0 copy-done.1
  12.2 2.1 multiply_convert_fusion
  14.2 0.0 all-gather.3.cloned.1.call-update
  14.3 0.0 reduce-scatter.2.cloned.1.call-start
  14.3 101.1 %all-gather.5.cloned.1.call-done = bf16[16,128,1920]{2,1,0:T(8,128)(2,1)} async-done(((bf16[1,128,1920]{2,1,0:T(8,128)(2,1)}), bf16[16,128,1920]{2,1,0:T(8,128)(2,1)}) %all-gather.5.cloned.1.call-update) | async-done | bytes 7864336 | tf_op jit(solution)/shard_map/all_gather | solution.py:20
  115.4 0.0 copy-done
  115.4 7.6 %fusion = bf16[16,128,4,120]{1,3,0,2:T(8,128)(2,1)} fusion(bf16[16,128,1920]{2,1,0:T(8,128)(2,1)} %all-gather.5.cloned.1.call-done, bf16[4,120,1920]{2,1,0:T(8,128)(2,1)S(1)} %copy-done), kind=kOutput, calls=%fused_computation | convolution fusion | flops 3774873600 | bytes 11673600 | tf_op jit(solution)/shard_map/qac,pdc->pqda/dot_general | solution.py:21
  123.0 91.3 %all-gather.3.cloned.1.call-done = bf16[16,120,1920]{2,1,0:T(8,128)(2,1)} async-done(((bf16[1,120,1920]{2,1,0:T(8,128)(2,1)}), bf16[16,120,1920]{2,1,0:T(8,128)(2,1)}) %all-gather.3.cloned.1.call-update) | async-done | bytes 7372816 | tf_op jit(solution)/shard_map/all_gather | solution.py:26
  214.3 9.8 %fusion.4 = f32[1920,4,128]{2,0,1:T(8,128)} fusion(bf16[16,120,1920]{2,1,0:T(8,128)(2,1)} %all-gather.3.cloned.1.call-done, bf16[16,128,4,120]{1,3,0,2:T(8,128)(2,1)} %fusion), kind=kOutput, calls=%fused_computation.4 | convolution fusion | flops 3774873600 | bytes 13271040 | tf_op jit(solution)/shard_map/qdb,pqda->bpa/dot_general | solution.py:24
  224.1 0.0 reduce-scatter.2.cloned.1.call-update
  224.1 97.2 %reduce-scatter.2.cloned.1.call-done = f32[120,4,128]{2,0,1:T(8,128)} async-done(((f32[1920,4,128]{2,0,1:T(8,128)}), f32[120,4,128]{2,0,1:T(8,128)}) %reduce-scatter.2.cloned.1.call-update) | async-done | bytes 245776 | tf_op jit(solution)/shard_map/reduce_scatter | solution.py:30
  321.2 1.7 copy.15
Async XLA Ops:
  6.5 108.9 %copy-start = (bf16[4,120,1920]{2,1,0:T(8,128)(2,1)S(1)}, bf16[4,120,1920]{2,1,0:T(8,128)(2,1)}, u32[]{:S(2)}) copy-start(bf16[4,120,1920]{2,1,0:T(8,128)(2,1)} %param.9) | copy-start | bytes 5529604
  6.5 5.6 %copy-start.1 = (bf16[1,120,1920]{2,1,0:T(8,128)(2,1)S(1)}, bf16[1,120,1920]{2,1,0:T(8,128)(2,1)}, u32[]{:S(2)}) copy-start(bf16[1,120,1920]{2,1,0:T(8,128)(2,1)} %param.7) | copy-start | bytes 1382404
  6.5 108.9 %all-gather.5.cloned.1.call-start = ((), (), s32[]{:S(2)}) async-start(), calls=%async_computation.2 | async-start | bytes 8355840 | tf_op jit(solution)/shard_map/all_gather | solution.py:20
  9.8 204.4 %all-gather.3.cloned.1.call-start = ((), (), s32[]{:S(2)}) async-start(), calls=%async_computation.1 | async-start | bytes 7833600 | tf_op jit(solution)/shard_map/all_gather | solution.py:26
  14.3 307.0 %reduce-scatter.2.cloned.1.call-start = ((), (), s32[]{:S(2)}) async-start(), calls=%async_computation.3 | async-start | bytes 4177920 | tf_op jit(solution)/shard_map/reduce_scatter | solution.py:30
Sparse Core Ops, SparseCore 0:
  10.1 105.2 all-gather.4
  118.1 96.0 all-gather.2
  224.2 96.9 reduce-scatter.1
where the time goes:
time: 330 us; the launch traced here: 329 us
  waiting for transfers between devices  290 us (88%)
  matrix products  17.4 us (5%)
  between operations  13.1 us (4%)
  local copies, waits for them, and re-layouts  7.14 us (2%)
    all_gather x1, waiting for transfers between devices, on_device(): row_all = lax.all_gather(row_local, 'aux', axis=0, tiled=True)  101 us
    reduce_scatter x1, waiting for transfers between devices, on_device(): return lax.psum_scatter(total, 'virt', scatter_dimension=0, tiled=True)  97.2 us
    all_gather x1, waiting for transfers between devices, on_device(): lax.all_gather(panel_local, 'aux', axis=0, tiled=True)  91.3 us
    dot_general x1, matrix products, on_device(): jnp.einsum('qdb,pqda->bpa', lax.all_gather(panel_local, 'aux', axis=0, ti...  9.79 us
    dot_general x1, matrix products, on_device(): jnp.einsum('qac,pdc->pqda', row_all, amplitudes, preferred_element_type=j...  7.57 us
  transfers between devices with their start and end apart: 3, of which 3 were waited for; matrix products, arithmetic and copies ran while one was open for 4% of the time, Pallas kernels for 0%

commit v1 on v0

--- a/solution.py
+++ b/solution.py
@@ -27,7 +27,11 @@
         half,
         preferred_element_type=jnp.float32,
     )
-    return lax.psum_scatter(total, "virt", scatter_dimension=0, tiled=True)
+    parts = lax.axis_size("virt")
+    width = total.shape[0] // parts
+    sent = total.astype(jnp.bfloat16).reshape(parts, width, *total.shape[1:])
+    got = lax.all_to_all(sent, "virt", 0, 0, tiled=True)
+    return got.astype(jnp.float32).sum(axis=0)
 
 
 def solution(mesh):

time: 330 us -> 283 us (0.86)
  waiting for transfers between devices: 290 us -> 193 us
  blocking collectives: 0 us -> 52 us
    reduce_scatter x1 -> x0, waiting for transfers between devices: 97.2 us -> none  [on_device(): return lax.psum_scatter(total, 'virt', scatter_dimension=0, tiled=True)]
    all_to_all x0 -> x1, blocking collectives: none -> 52 us  [on_device(): got = lax.all_to_all(sent, 'virt', 0, 0, tiled=True)]
  transfers between devices with their start and end apart: 3 -> 2, of which waited for: 3 -> 2; matrix products, arithmetic and copies ran while one was open for 4% -> 4% of each run, Pallas kernels for 0% -> 0%
where the time goes in v1:
time: 283 us; the launch traced here: 282 us
  waiting for transfers between devices  193 us (68%)
  blocking collectives  52 us (18%)
  matrix products  15.5 us (5%)
  between operations  13.4 us (5%)
  local copies, waits for them, and re-layouts  5.68 us (2%)
    all_gather x1, waiting for transfers between devices, on_device(): row_all = lax.all_gather(row_local, 'aux', axis=0, tiled=True)  102 us
    all_gather x1, waiting for transfers between devices, on_device(): lax.all_gather(panel_local, 'aux', axis=0, tiled=True)  91.3 us
    all_to_all x1, blocking collectives, on_device(): got = lax.all_to_all(sent, 'virt', 0, 0, tiled=True)  52 us
    dot_general x1, matrix products, on_device(): jnp.einsum('qdb,pqda->bpa', lax.all_gather(panel_local, 'aux', axis=0, ti...  7.93 us
    dot_general x1, matrix products, on_device(): jnp.einsum('qac,pdc->pqda', row_all, amplitudes, preferred_element_type=j...  7.58 us
  transfers between devices with their start and end apart: 2, of which 2 were waited for; matrix products, arithmetic and copies ran while one was open for 4% of the time, Pallas kernels for 0%

profile of v1, /device:TPU:8, one launch (start us, length us, event | category | flops | bytes accessed | tf_op | source)
XLA Modules:
  0.0 282.2 jit_solution(2176441947941358192)
XLA Ops:
  6.5 0.0 copy-start
  6.5 0.0 copy-start.2
  6.5 0.0 all-gather.5.cloned.1.call-start
  6.5 0.8 copy.22
  7.4 1.3 copy.11
  8.7 0.1 fusion.9
  8.8 1.0 copy.12
  9.8 0.0 copy-start.1
  9.8 0.0 all-gather.5.cloned.1.call-update
  9.8 0.0 all-gather.3.cloned.1.call-start
  9.9 0.0 copy-done.2
  9.9 0.1 copy.18
  10.0 0.3 mul.33
  10.3 1.2 mul.34
  11.5 0.0 copy-done.1
  11.5 2.0 multiply_convert_fusion
  13.5 0.0 all-gather.3.cloned.1.call-update
  13.6 101.8 %all-gather.5.cloned.1.call-done = bf16[16,128,1920]{2,1,0:T(8,128)(2,1)} async-done(((bf16[1,128,1920]{2,1,0:T(8,128)(2,1)}), bf16[16,128,1920]{2,1,0:T(8,128)(2,1)}) %all-gather.5.cloned.1.call-update) | async-done | bytes 7864336 | tf_op jit(solution)/shard_map/all_gather | solution.py:20
  115.4 0.0 copy-done
  115.4 7.6 %fusion = bf16[16,128,4,120]{1,3,0,2:T(8,128)(2,1)} fusion(bf16[16,128,1920]{2,1,0:T(8,128)(2,1)} %all-gather.5.cloned.1.call-done, bf16[4,120,1920]{2,1,0:T(8,128)(2,1)S(1)} %copy-done), kind=kOutput, calls=%fused_computation | convolution fusion | flops 3774873600 | bytes 11673600 | tf_op jit(solution)/shard_map/qac,pdc->pqda/dot_general | solution.py:21
  123.0 91.3 %all-gather.3.cloned.1.call-done = bf16[16,120,1920]{2,1,0:T(8,128)(2,1)} async-done(((bf16[1,120,1920]{2,1,0:T(8,128)(2,1)}), bf16[16,120,1920]{2,1,0:T(8,128)(2,1)}) %all-gather.3.cloned.1.call-update) | async-done | bytes 7372816 | tf_op jit(solution)/shard_map/all_gather | solution.py:26
  214.3 7.9 %bitcast_convert_fusion = bf16[1920,4,128]{2,0,1:T(8,128)(2,1)S(1)} fusion(bf16[16,120,1920]{2,1,0:T(8,128)(2,1)} %all-gather.3.cloned.1.call-done, bf16[16,128,4,120]{1,3,0,2:T(8,128)(2,1)} %fusion), kind=kOutput, calls=%fused_computation.4 | convolution fusion | flops 3775856640 | bytes 11304960 | tf_op jit(solution)/shard_map/qdb,pqda->bpa/dot_general | solution.py:24
  222.2 0.1 copy.13
  222.4 52.0 %all_to_all.5 = bf16[16,120,4,128]{3,1,2,0:T(8,128)(2,1)S(1)} all-to-all(bf16[16,120,4,128]{3,1,2,0:T(8,128)(2,1)S(1)} %copy.13), channel_id=1, replica_groups=mesh['aux'=16,'virt'=16] {'virt'}, dimensions={0} | all-to-all | bytes 3932160 | tf_op jit(solution)/shard_map/all_to_all | solution.py:33
  274.3 0.3 convert_reduce_fusion
  274.6 0.8 copy.15
Async XLA Ops:
  6.5 108.9 %copy-start = (bf16[4,120,1920]{2,1,0:T(8,128)(2,1)S(1)}, bf16[4,120,1920]{2,1,0:T(8,128)(2,1)}, u32[]{:S(2)}) copy-start(bf16[4,120,1920]{2,1,0:T(8,128)(2,1)} %param.9) | copy-start | bytes 5529604
  6.5 3.4 %copy-start.2 = (f32[1,120,15]{1,0,2:T(1,128)S(1)}, f32[1,120,15]{1,0,2:T(1,128)}, u32[]{:S(2)}) copy-start(f32[1,120,15]{1,0,2:T(1,128)} %param.8) | copy-start | bytes 21604
  6.5 108.9 %all-gather.5.cloned.1.call-start = ((), (), s32[]{:S(2)}) async-start(), calls=%async_computation.2 | async-start | bytes 8355840 | tf_op jit(solution)/shard_map/all_gather | solution.py:20
  9.8 1.7 copy-start.1
  9.8 204.4 %all-gather.3.cloned.1.call-start = ((), (), s32[]{:S(2)}) async-start(), calls=%async_computation.1 | async-start | bytes 7833600 | tf_op jit(solution)/shard_map/all_gather | solution.py:26
Sparse Core Ops, SparseCore 0:
  10.1 105.2 all-gather.4
  118.1 96.0 all-gather.2

commit v2 on v1

--- a/solution.py
+++ b/solution.py
@@ -17,15 +17,17 @@
 def on_device(row_codes, row_scales, panel_codes, panel_scales, amplitudes):
     row_local = decode_rows(row_codes, row_scales)
     panel_local = decode_rows(panel_codes, panel_scales)
-    row_all = lax.all_gather(row_local, "aux", axis=0, tiled=True)
+    rows = row_local.shape[1]
+    both = lax.all_gather(
+        jnp.concatenate([row_local, panel_local], axis=1), "aux", axis=0, tiled=True
+    )
+    row_all = both[:, :rows]
+    panel_all = both[:, rows:]
     half = jnp.einsum(
         "qac,pdc->pqda", row_all, amplitudes, preferred_element_type=jnp.float32
     ).astype(jnp.bfloat16)
     total = jnp.einsum(
-        "qdb,pqda->bpa",
-        lax.all_gather(panel_local, "aux", axis=0, tiled=True),
-        half,
-        preferred_element_type=jnp.float32,
+        "qdb,pqda->bpa", panel_all, half, preferred_element_type=jnp.float32
     )
     parts = lax.axis_size("virt")
     width = total.shape[0] // parts

time: 283 us -> 251 us (0.89)
  waiting for transfers between devices: 193 us -> 163 us
  matrix products: 15.5 us -> 11.1 us
    all_gather x2 -> x1, waiting for transfers between devices: 193 us -> 163 us  [on_device(): lax.all_gather(jnp.concatenate([row_local, panel_local], axis=1), 'aux',...]
    dot_general x1, matrix products: 7.93 us -> 4.28 us  [on_device(): jnp.einsum('qdb,pqda->bpa', panel_all, half, preferred_element_type=jnp.f...]
  transfers between devices with their start and end apart: 2 -> 1, of which waited for: 2 -> 1; matrix products, arithmetic and copies ran while one was open for 4% -> 0% of each run, Pallas kernels for 0% -> 0%
where the time goes in v2:
time: 251 us; the launch traced here: 249 us
  waiting for transfers between devices  163 us (65%)
  blocking collectives  52.2 us (21%)
  between operations  13.5 us (5%)
  matrix products  11.1 us (4%)
  local copies, waits for them, and re-layouts  7.75 us (3%)
    all_gather x1, waiting for transfers between devices, on_device(): lax.all_gather(jnp.concatenate([row_local, panel_local], axis=1), 'aux',...  163 us
    all_to_all x1, blocking collectives, on_device(): got = lax.all_to_all(sent, 'virt', 0, 0, tiled=True)  52.2 us
    dot_general x1, matrix products, on_device(): jnp.einsum('qac,pdc->pqda', row_all, amplitudes, preferred_element_type=j...  6.78 us
  transfers between devices with their start and end apart: 1, of which 1 were waited for; matrix products, arithmetic and copies ran while one was open for 0% of the time, Pallas kernels for 0%

profile of v2, /device:TPU:8, one launch (start us, length us, event | category | flops | bytes accessed | tf_op | source)
XLA Modules:
  0.0 249.3 jit_solution(2272180668760890021)
XLA Ops:
  6.5 0.0 copy-start
  6.5 0.0 all-gather.2.cloned.1.call-start
  6.5 0.8 copy.31
  7.4 0.8 copy.27
  8.2 1.3 copy.18
  9.5 0.3 mul.37
  9.8 1.1 mul.38
  10.9 1.4 multiply_convert_fusion
  12.2 0.3 copy.20
  12.5 0.1 fusion.5
  12.6 0.2 pad_maximum_fusion
  12.8 1.4 copy.21
  14.2 0.0 all-gather.2.cloned.1.call-update
  14.3 162.8 %all-gather.2.cloned.1.call-done = bf16[16,248,1920]{2,1,0:T(8,128)(2,1)} async-done(((bf16[1,248,1920]{2,1,0:T(8,128)(2,1)}), bf16[16,248,1920]{2,1,0:T(8,128)(2,1)}) %all-gather.2.cloned.1.call-update) | async-done | bytes 15237136 | tf_op jit(solution)/shard_map/all_gather | solution.py:21
  177.1 0.0 copy-done
  177.1 0.0 copy-start.1
  177.1 6.8 %fusion = bf16[16,128,4,120]{1,3,0,2:T(8,128)(2,1)S(1)} fusion(bf16[16,248,1920]{2,1,0:T(8,128)(2,1)} %all-gather.2.cloned.1.call-done, bf16[4,120,1920]{2,1,0:T(8,128)(2,1)S(1)} %copy-done), kind=kOutput, calls=%fused_computation.1 | convolution fusion | flops 3774873600 | bytes 11673600 | tf_op jit(solution)/shard_map/qac,pdc->pqda/dot_general | solution.py:26
  183.9 0.8 copy-done.1
  184.7 4.3 %bitcast_convert_fusion = bf16[1920,4,128]{2,0,1:T(8,128)(2,1)S(1)} fusion(bf16[16,248,1920]{2,1,0:T(8,128)(2,1)S(1)} %copy-done.1, bf16[16,128,4,120]{1,3,0,2:T(8,128)(2,1)S(1)} %fusion), kind=kOutput, calls=%fused_computation.4 | convolution fusion | flops 3775856640 | bytes 11304960 | tf_op jit(solution)/shard_map/qdb,pqda->bpa/dot_general | solution.py:29
  189.0 0.2 copy.22
  189.2 52.2 %all_to_all.5 = bf16[16,120,4,128]{3,1,2,0:T(8,128)(2,1)S(1)} all-to-all(bf16[16,120,4,128]{3,1,2,0:T(8,128)(2,1)S(1)} %copy.22), channel_id=1, replica_groups=mesh['aux'=16,'virt'=16] {'virt'}, dimensions={0} | all-to-all | bytes 3932160 | tf_op jit(solution)/shard_map/all_to_all | solution.py:35
  241.4 0.3 convert_reduce_fusion
  241.7 0.8 copy.24
Async XLA Ops:
  6.5 170.5 %copy-start = (bf16[4,120,1920]{2,1,0:T(8,128)(2,1)S(1)}, bf16[4,120,1920]{2,1,0:T(8,128)(2,1)}, u32[]{:S(2)}) copy-start(bf16[4,120,1920]{2,1,0:T(8,128)(2,1)} %param.9) | copy-start | bytes 5529604
  6.5 170.5 %all-gather.2.cloned.1.call-start = ((), (), s32[]{:S(2)}) async-start(), calls=%async_computation.1 | async-start | bytes 16189440 | tf_op jit(solution)/shard_map/all_gather | solution.py:21
  177.1 7.6 %copy-start.1 = (bf16[16,248,1920]{2,1,0:T(8,128)(2,1)S(1)}, bf16[16,248,1920]{2,1,0:T(8,128)(2,1)}, u32[]{:S(2)}) copy-start(bf16[16,248,1920]{2,1,0:T(8,128)(2,1)} %all-gather.2.cloned.1.call-done) | copy-start | bytes 45711364
Sparse Core Ops, SparseCore 0:
  14.4 162.6 all-gather.1

commit v3 on v2

v3 whole, which is shorter than its diff:
```python
import jax
import jax.numpy as jnp
from jax import lax
from jax.sharding import Mesh
from jax.sharding import PartitionSpec as P

AUX = ("z_hi", "y", "core")
VIRT = ("x", "z_lo")


def decode_rows(codes, scales):
    count, width, length = codes.shape
    blocks = scales.shape[2]
    wide = (
        codes.astype(jnp.float32).reshape(count, width, blocks, length // blocks)
        * scales[:, :, :, None]
    )
    return wide.reshape(count, width, length).astype(jnp.bfloat16)


def on_device(row_codes, row_scales, panel_codes, panel_scales, amplitudes):
    row_local = decode_rows(row_codes, row_scales)
    panel_local = decode_rows(panel_codes, panel_scales)
    rows = row_local.shape[1]
    mine = jnp.concatenate([row_local, panel_local], axis=1)
    halves = lax.axis_size("z_hi")
    other = lax.ppermute(mine, "z_hi", [(i, (i + 1) % halves) for i in range(halves)])
    both = lax.all_gather(
        jnp.stack([mine, other], axis=1), ("y", "core"), axis=0, tiled=True
    )
    row_all = both[:, :, :rows]
    panel_all = both[:, :, rows:]
    half = jnp.einsum(
        "gsac,pdc->pgsda", row_all, amplitudes, preferred_element_type=jnp.float32
    ).astype(jnp.bfloat16)
    total = jnp.einsum(
        "gsdb,pgsda->bpa", panel_all, half, preferred_element_type=jnp.float32
    )
    parts = lax.axis_size(VIRT)
    width = total.shape[0] // parts
    sent = total.astype(jnp.bfloat16).reshape(parts, width, *total.shape[1:])
    got = lax.all_to_all(sent, VIRT, 0, 0, tiled=True)
    return got.astype(jnp.float32).sum(axis=0)


def solution(mesh):
    sizes = dict(z_hi=2, y=4, core=2, x=4, z_lo=4)
    fine = Mesh(mesh.devices.reshape([sizes[n] for n in AUX + VIRT]), AUX + VIRT)
    placed = (
        P(AUX, None, None),
        P(AUX, None, None),
        P(AUX, VIRT, None),
        P(AUX, VIRT, None),
        P(AUX, VIRT, None),
    )
    return jax.shard_map(
        on_device, mesh=fine, in_specs=placed, out_specs=P(VIRT, AUX, None), check_vma=False
    )
```

time: 251 us -> 230 us (0.916)
  waiting for transfers between devices: 163 us -> 123 us
  starting transfers between devices: 0.01 us -> 7.19 us
  local copies, waits for them, and re-layouts: 7.75 us -> 13.3 us
  other arithmetic: 1.94 us -> 5.79 us
  blocking collectives: 52.2 us -> 54.9 us
    all_gather x1, waiting for transfers between devices: 163 us -> 82.9 us  [on_device(): lax.all_gather(jnp.stack([mine, other], axis=1), ('y', 'core'), axis=0, t...]
    ppermute x0 -> x1, waiting for transfers between devices: none -> 40.5 us  [on_device(): lax.ppermute(mine, 'z_hi', [(i, (i + 1) % halves) for i in range(halves)])]
    ppermute x0 -> x1, starting transfers between devices: none -> 7.19 us  [on_device(): lax.ppermute(mine, 'z_hi', [(i, (i + 1) % halves) for i in range(halves)])]
    another operation x0 -> x2, other arithmetic: none -> 4.03 us  [on_device(): jnp.stack([mine, other], axis=1)]
    another operation x0 -> x1, local copies, waits for them, and re-layouts: none -> 4 us  [on_device(): jnp.stack([mine, other], axis=1)]
    all_to_all x1, blocking collectives: 52.2 us -> 54.9 us  [on_device(): got = lax.all_to_all(sent, VIRT, 0, 0, tiled=True)]
  transfers between devices with their start and end apart: 1 -> 2, of which waited for: 1 -> 2; matrix products, arithmetic and copies ran while one was open for 0% -> 0% of each run, Pallas kernels for 0% -> 0%
where the time goes in v3:
time: 230 us; the launch traced here: 229 us
  waiting for transfers between devices  123 us (53%)
  blocking collectives  54.9 us (24%)
  between operations  13.5 us (6%)
  local copies, waits for them, and re-layouts  13.3 us (6%)
  matrix products  11 us (5%)
  starting transfers between devices  7.19 us (3%)
  other arithmetic  5.79 us (3%)
    all_gather x1, waiting for transfers between devices, on_device(): lax.all_gather(jnp.stack([mine, other], axis=1), ('y', 'core'), axis=0, t...  82.9 us
    all_to_all x1, blocking collectives, on_device(): got = lax.all_to_all(sent, VIRT, 0, 0, tiled=True)  54.9 us
    ppermute x1, waiting for transfers between devices, on_device(): lax.ppermute(mine, 'z_hi', [(i, (i + 1) % halves) for i in range(halves)])  40.5 us
    ppermute x1, starting transfers between devices, on_device(): lax.ppermute(mine, 'z_hi', [(i, (i + 1) % halves) for i in range(halves)])  7.19 us
    dot_general x1, matrix products, on_device(): jnp.einsum('gsac,pdc->pgsda', row_all, amplitudes, preferred_element_type...  6.77 us
  transfers between devices with their start and end apart: 2, of which 2 were waited for; matrix products, arithmetic and copies ran while one was open for 0% of the time, Pallas kernels for 0%

profile of v3, /device:TPU:8, one launch (start us, length us, event | category | flops | bytes accessed | tf_op | source)
XLA Modules:
  0.0 229.2 jit_solution(9776517771293870650)
XLA Ops:
  6.5 0.0 copy-start
  6.5 0.0 all-gather.2.cloned.1.call-start
  6.5 0.8 copy.47
  7.4 0.8 copy.43
  8.2 1.3 copy.30
  9.5 0.3 mul.37
  9.8 1.1 mul.38
  10.9 1.4 multiply_convert_fusion
  12.2 0.3 copy.32
  12.5 0.1 fusion.5
  12.6 1.2 fusion.6
  13.8 1.4 copy.33
  15.2 7.2 %collective-permute-start = (bf16[1,248,1920]{2,1,0:T(8,128)(2,1)}, bf16[1,248,1920]{2,1,0:T(8,128)(2,1)}, u32[]{:S(2)}, u32[]{:S(2)}) collective-permute-start(bf16[1,248,1920]{2,1,0:T(8,128)(2,1)} %copy.33), channel_id=1, source_target_pairs={{0,128},{128,0},{1,129},{129,1},{2,130},{130,2},{3,131},{131,3},{4... | collective-permute-start | bytes 2856968 | tf_op jit(solution)/shard_map/ppermute | solution.py:27
  22.4 40.5 %collective-permute-done = bf16[1,248,1920]{2,1,0:T(8,128)(2,1)} collective-permute-done((bf16[1,248,1920]{2,1,0:T(8,128)(2,1)}, bf16[1,248,1920]{2,1,0:T(8,128)(2,1)}, u32[]{:S(2)}, u32[]{:S(2)}) %collective-permute-start) | collective-permute-done | bytes 952352 | tf_op jit(solution)/shard_map/ppermute | solution.py:27
  62.9 1.6 copy.34
  64.5 2.9 %pad_maximum_fusion = bf16[1,2,248,1920]{2,3,1,0:T(8,128)(2,1)} fusion(bf16[1,1,248,1920]{2,3,1,0:T(8,128)(2,1)S(1)} %bitcast.38, bf16[1,1,248,1920]{2,3,1,0:T(8,128)(2,1)} %get-tuple-element.5), kind=kLoop, calls=%fused_computation.6 | loop fusion | flops 952320 | bytes 3809280 | tf_op jit(solution)/shard_map/stack | solution.py:29
  67.4 4.0 %copy.35 = bf16[1,2,248,1920]{3,2,1,0:T(8,128)(2,1)} copy(bf16[1,2,248,1920]{2,3,1,0:T(8,128)(2,1)} %pad_maximum_fusion) | data formatting | bytes 3809280 | tf_op jit(solution)/shard_map/stack | solution.py:29
  71.4 0.0 all-gather.2.cloned.1.call-update
  71.4 82.9 %all-gather.2.cloned.1.call-done = bf16[8,2,248,1920]{3,2,1,0:T(8,128)(2,1)} async-done(((bf16[1,2,248,1920]{3,2,1,0:T(8,128)(2,1)}), bf16[8,2,248,1920]{3,2,1,0:T(8,128)(2,1)}) %all-gather.2.cloned.1.call-update) | async-done | bytes 15237136 | tf_op jit(solution)/shard_map/all_gather | solution.py:28
  154.3 0.0 copy-done
  154.3 0.0 copy-start.1
  154.3 6.8 %fusion = bf16[8,2,128,4,120]{2,4,1,0,3:T(8,128)(2,1)S(1)} fusion(bf16[8,2,248,1920]{3,2,1,0:T(8,128)(2,1)} %all-gather.2.cloned.1.call-done, bf16[4,120,1920]{2,1,0:T(8,128)(2,1)S(1)} %copy-done), kind=kOutput, calls=%fused_computation.1 | convolution fusion | flops 3774873600 | bytes 11673600 | tf_op jit(solution)/shard_map/gsac,pdc->pgsda/dot_general | solution.py:33
  161.1 0.9 copy-done.1
  161.9 4.3 %bitcast_convert_fusion = bf16[1920,4,128]{2,0,1:T(8,128)(2,1)S(1)} fusion(bf16[8,2,248,1920]{3,2,1,0:T(8,128)(2,1)S(1)} %copy-done.1, bf16[8,2,128,4,120]{2,4,1,0,3:T(8,128)(2,1)S(1)} %fusion), kind=kOutput, calls=%fused_computation.4 | convolution fusion | flops 3775856640 | bytes 11304960 | tf_op jit(solution)/shard_map/gsdb,pgsda->bpa/dot_general | solution.py:36
  166.2 0.2 copy.37
  166.4 54.9 %all_to_all.5 = bf16[16,120,4,128]{3,1,2,0:T(8,128)(2,1)S(1)} all-to-all(bf16[16,120,4,128]{3,1,2,0:T(8,128)(2,1)S(1)} %copy.37), channel_id=1, replica_groups=mesh['z_hi'=2,'y'=4,'core'=2,'x'=4,'z_lo'=4] {'x','z_lo'}, dimensions={0} | all-to-all | bytes 3932160 | tf_op jit(solution)/shard_map/all_to_all | solution.py:42
  221.3 0.3 convert_reduce_fusion
  221.6 0.8 copy.39
Async XLA Ops:
  6.5 147.8 %copy-start = (bf16[4,120,1920]{2,1,0:T(8,128)(2,1)S(1)}, bf16[4,120,1920]{2,1,0:T(8,128)(2,1)}, u32[]{:S(2)}) copy-start(bf16[4,120,1920]{2,1,0:T(8,128)(2,1)} %param.9) | copy-start | bytes 5529604
  6.5 147.8 %all-gather.2.cloned.1.call-start = ((), (), s32[]{:S(2)}) async-start(), calls=%async_computation.1 | async-start | bytes 17141760 | tf_op jit(solution)/shard_map/all_gather | solution.py:28
  15.2 47.7 %collective-permute-start = (bf16[1,248,1920]{2,1,0:T(8,128)(2,1)}, bf16[1,248,1920]{2,1,0:T(8,128)(2,1)}, u32[]{:S(2)}, u32[]{:S(2)}) collective-permute-start(bf16[1,248,1920]{2,1,0:T(8,128)(2,1)} %copy.33), channel_id=1, source_target_pairs={{0,128},{128,0},{1,129},{129,1},{2,130},{130,2},{3,131},{131,3},{4... | collective-permute-start | bytes 2856968 | tf_op jit(solution)/shard_map/ppermute | solution.py:27
  154.3 7.6 %copy-start.1 = (bf16[8,2,248,1920]{3,2,1,0:T(8,128)(2,1)S(1)}, bf16[8,2,248,1920]{3,2,1,0:T(8,128)(2,1)}, u32[]{:S(2)}) copy-start(bf16[8,2,248,1920]{3,2,1,0:T(8,128)(2,1)} %all-gather.2.cloned.1.call-done) | copy-start | bytes 45711364
Sparse Core Ops, SparseCore 0:
  71.5 82.7 all-gather.1

commit v4 on v3

--- a/solution.py
+++ b/solution.py
@@ -25,17 +25,16 @@
     mine = jnp.concatenate([row_local, panel_local], axis=1)
     halves = lax.axis_size("z_hi")
     other = lax.ppermute(mine, "z_hi", [(i, (i + 1) % halves) for i in range(halves)])
-    both = lax.all_gather(
-        jnp.stack([mine, other], axis=1), ("y", "core"), axis=0, tiled=True
-    )
-    row_all = both[:, :, :rows]
-    panel_all = both[:, :, rows:]
-    half = jnp.einsum(
-        "gsac,pdc->pgsda", row_all, amplitudes, preferred_element_type=jnp.float32
-    ).astype(jnp.bfloat16)
-    total = jnp.einsum(
-        "gsdb,pgsda->bpa", panel_all, half, preferred_element_type=jnp.float32
-    )
+    total = None
+    for blocks in (mine, other):
+        gathered = lax.all_gather(blocks, ("y", "core"), axis=0, tiled=True)
+        half = jnp.einsum(
+            "qac,pdc->pqda", gathered[:, :rows], amplitudes, preferred_element_type=jnp.float32
+        ).astype(jnp.bfloat16)
+        part = jnp.einsum(
+            "qdb,pqda->bpa", gathered[:, rows:], half, preferred_element_type=jnp.float32
+        )
+        total = part if total is None else total + part
     parts = lax.axis_size(VIRT)
     width = total.shape[0] // parts
     sent = total.astype(jnp.bfloat16).reshape(parts, width, *total.shape[1:])

time: 230 us -> 192 us (0.83)
  waiting for transfers between devices: 123 us -> 84.5 us
  matrix products: 11 us -> 19.4 us
  local copies, waits for them, and re-layouts: 13.3 us -> 9.4 us
  other arithmetic: 5.79 us -> 1.94 us
    all_gather x1 -> x2, waiting for transfers between devices: 82.9 us -> 44 us  [on_device(): gathered = lax.all_gather(blocks, ('y', 'core'), axis=0, tiled=True)]
    dot_general x2, matrix products: 11 us -> 19.4 us  [on_device(): jnp.einsum('qdb,pqda->bpa', gathered[:, rows:], half, preferred_element_t...]
    another operation x2 -> x0, other arithmetic: 4.03 us -> none  [on_device(): jnp.stack([mine, other], axis=1)]
    another operation x1 -> x0, local copies, waits for them, and re-layouts: 4 us -> none  [on_device(): jnp.stack([mine, other], axis=1)]
  transfers between devices with their start and end apart: 2 -> 3, of which waited for: 2 -> 3; matrix products, arithmetic and copies ran while one was open for 0% -> 5% of each run, Pallas kernels for 0% -> 0%
where the time goes in v4:
time: 192 us; the launch traced here: 191 us
  waiting for transfers between devices  84.5 us (44%)
  blocking collectives  54.9 us (29%)
  matrix products  19.4 us (10%)
  between operations  13.4 us (7%)
  local copies, waits for them, and re-layouts  9.4 us (5%)
  starting transfers between devices  7.32 us (4%)
  other arithmetic  1.94 us (1%)
    all_to_all x1, blocking collectives, on_device(): got = lax.all_to_all(sent, VIRT, 0, 0, tiled=True)  54.9 us
    all_gather x2, waiting for transfers between devices, on_device(): gathered = lax.all_gather(blocks, ('y', 'core'), axis=0, tiled=True)  44 us
    ppermute x1, waiting for transfers between devices, on_device(): lax.ppermute(mine, 'z_hi', [(i, (i + 1) % halves) for i in range(halves)])  40.5 us
    dot_general x2, matrix products, on_device(): jnp.einsum('qdb,pqda->bpa', gathered[:, rows:], half, preferred_element_t...  19.4 us
    ppermute x1, starting transfers between devices, on_device(): lax.ppermute(mine, 'z_hi', [(i, (i + 1) % halves) for i in range(halves)])  7.28 us
  transfers between devices with their start and end apart: 3, of which 3 were waited for; matrix products, arithmetic and copies ran while one was open for 5% of the time, Pallas kernels for 0%

profile of v4, /device:TPU:8, one launch (start us, length us, event | category | flops | bytes accessed | tf_op | source)
XLA Modules:
  0.0 191.0 jit_solution(15582170708850478409)
XLA Ops:
  6.5 0.0 copy-start
  6.5 0.0 all-gather.3.cloned.1.call-start
  6.5 0.8 copy.43
  7.4 0.8 copy.39
  8.2 1.3 copy.28
  9.5 0.3 mul.37
  9.8 1.1 mul.38
  10.9 1.4 multiply_convert_fusion
  12.3 0.3 copy.30
  12.6 0.1 fusion.19
  12.7 0.2 pad_maximum_fusion
  12.9 1.4 copy.31
  14.2 0.0 all-gather.3.cloned.1.call-update
  14.3 0.0 all-gather.5.cloned.1.call-start
  14.3 7.3 %collective-permute-start = (bf16[1,248,1920]{2,1,0:T(8,128)(2,1)}, bf16[1,248,1920]{2,1,0:T(8,128)(2,1)S(1)}, u32[]{:S(2)}, u32[]{:S(2)}) collective-permute-start(bf16[1,248,1920]{2,1,0:T(8,128)(2,1)} %copy.31), channel_id=1, source_target_pairs={{0,128},{128,0},{1,129},{129,1},{2,130},{130,2},{3,131},{131,3},{4... | collective-permute-start | bytes 2856968 | tf_op jit(solution)/shard_map/ppermute | solution.py:27
  21.6 40.5 %collective-permute-done = bf16[1,248,1920]{2,1,0:T(8,128)(2,1)S(1)} collective-permute-done((bf16[1,248,1920]{2,1,0:T(8,128)(2,1)}, bf16[1,248,1920]{2,1,0:T(8,128)(2,1)S(1)}, u32[]{:S(2)}, u32[]{:S(2)}) %collective-permute-start) | collective-permute-done | bytes 952352 | tf_op jit(solution)/shard_map/ppermute | solution.py:27
  62.1 0.0 copy-start.1
  62.1 0.9 copy-done.1
  63.1 0.0 all-gather.5.cloned.1.call-update
  63.1 2.3 %all-gather.3.cloned.1.call-done = bf16[8,248,1920]{2,1,0:T(8,128)(2,1)} async-done(((bf16[1,248,1920]{2,1,0:T(8,128)(2,1)}), bf16[8,248,1920]{2,1,0:T(8,128)(2,1)}) %all-gather.3.cloned.1.call-update) | async-done | bytes 7618576 | tf_op jit(solution)/shard_map/all_gather | solution.py:30
  65.4 0.0 copy-done
  65.4 9.4 %fusion.4 = f32[1920,4,128,1]{2,0,3,1:T(8,128)} fusion(bf16[8,248,1920]{2,1,0:T(8,128)(2,1)} %all-gather.3.cloned.1.call-done, bf16[4,120,1920]{2,1,0:T(8,128)(2,1)S(1)} %copy-done), kind=kOutput, calls=%fused_computation.10 | convolution fusion | flops 3775365120 | bytes 13393920 | tf_op jit(solution)/shard_map/qdb,pqda->bpa/dot_general | solution.py:34
  74.9 41.6 %all-gather.5.cloned.1.call-done = bf16[8,248,1920]{2,1,0:T(8,128)(2,1)} async-done(((bf16[1,248,1920]{2,1,0:T(8,128)(2,1)}), bf16[8,248,1920]{2,1,0:T(8,128)(2,1)}) %all-gather.5.cloned.1.call-update) | async-done | bytes 7618576 | tf_op jit(solution)/shard_map/all_gather | solution.py:30
  116.5 10.0 %fusion.2 = bf16[1920,4,128]{2,0,1:T(8,128)(2,1)} fusion(f32[1920,4,128,1]{2,0,3,1:T(8,128)} %fusion.4, bf16[8,248,1920]{2,1,0:T(8,128)(2,1)} %all-gather.5.cloned.1.call-done, bf16[4,120,1920]{2,1,0:T(8,128)(2,1)S(1)} %copy-done), kind=kOutput, calls=%fused_computation.5 | convolution fusion | flops 3777331200 | bytes 15360000 | tf_op jit(solution)/shard_map/qdb,pqda->bpa/dot_general | solution.py:34
  126.5 1.7 copy.33
  128.2 54.9 %all_to_all.5 = bf16[16,120,4,128]{3,1,2,0:T(8,128)(2,1)S(1)} all-to-all(bf16[16,120,4,128]{3,1,2,0:T(8,128)(2,1)S(1)} %copy.33), channel_id=1, replica_groups=mesh['z_hi'=2,'y'=4,'core'=2,'x'=4,'z_lo'=4] {'x','z_lo'}, dimensions={0} | all-to-all | bytes 3932160 | tf_op jit(solution)/shard_map/all_to_all | solution.py:41
  183.1 0.3 convert_reduce_fusion
  183.4 0.8 copy.35
Async XLA Ops:
  6.5 58.9 %copy-start = (bf16[4,120,1920]{2,1,0:T(8,128)(2,1)S(1)}, bf16[4,120,1920]{2,1,0:T(8,128)(2,1)}, u32[]{:S(2)}) copy-start(bf16[4,120,1920]{2,1,0:T(8,128)(2,1)} %param.9) | copy-start | bytes 5529604
  6.5 58.9 %all-gather.3.cloned.1.call-start = ((), (), s32[]{:S(2)}) async-start(), calls=%async_computation.1 | async-start | bytes 8570880 | tf_op jit(solution)/shard_map/all_gather | solution.py:30
  14.3 102.2 %all-gather.5.cloned.1.call-start = ((), (), s32[]{:S(2)}) async-start(), calls=%async_computation.2 | async-start | bytes 8570880 | tf_op jit(solution)/shard_map/all_gather | solution.py:30
  14.3 47.8 %collective-permute-start = (bf16[1,248,1920]{2,1,0:T(8,128)(2,1)}, bf16[1,248,1920]{2,1,0:T(8,128)(2,1)S(1)}, u32[]{:S(2)}, u32[]{:S(2)}) collective-permute-start(bf16[1,248,1920]{2,1,0:T(8,128)(2,1)} %copy.31), channel_id=1, source_target_pairs={{0,128},{128,0},{1,129},{129,1},{2,130},{130,2},{3,131},{131,3},{4... | collective-permute-start | bytes 2856968 | tf_op jit(solution)/shard_map/ppermute | solution.py:27
  62.1 0.9 copy-start.1
Sparse Core Ops, SparseCore 0:
  14.4 51.0 all-gather.2
  67.3 49.1 all-gather.4

commit v5 on v4

--- a/solution.py
+++ b/solution.py
@@ -35,12 +35,13 @@
             "qdb,pqda->bpa", gathered[:, rows:], half, preferred_element_type=jnp.float32
         )
         total = part if total is None else total + part
-    parts = lax.axis_size(VIRT)
-    width = total.shape[0] // parts
-    sent = total.astype(jnp.bfloat16).reshape(parts, width, *total.shape[1:])
-    got = lax.all_to_all(sent, VIRT, 0, 0, tiled=True)
+    across, along = lax.axis_size("x"), lax.axis_size("z_lo")
+    width = total.shape[0] // (across * along)
+    sent = total.astype(jnp.bfloat16).reshape(across, along, width, *total.shape[1:])
+    got = lax.all_to_all(sent, "x", 0, 0, tiled=True)
+    summed = got.astype(jnp.float32).sum(axis=0).astype(jnp.bfloat16)
+    got = lax.all_to_all(summed, "z_lo", 0, 0, tiled=True)
     return got.astype(jnp.float32).sum(axis=0)
-
 
 def solution(mesh):
     sizes = dict(z_hi=2, y=4, core=2, x=4, z_lo=4)

time: 192 us -> 188 us (0.979)
  blocking collectives: 54.9 us -> 47.1 us
  other arithmetic: 1.94 us -> 4.65 us
    all_to_all x1 -> x2, blocking collectives: 54.9 us -> 47.1 us  [the longest x1 29.5 us: on_device(): got = lax.all_to_all(sent, 'x', 0, 0, tiled=True)]
where the time goes in v5:
time: 188 us; the launch traced here: 187 us
  waiting for transfers between devices  84.5 us (45%)
  blocking collectives  47.1 us (25%)
  matrix products  19.4 us (10%)
  between operations  13.4 us (7%)
  local copies, waits for them, and re-layouts  10.2 us (5%)
  starting transfers between devices  7.32 us (4%)
  other arithmetic  4.65 us (2%)
    all_gather x2, waiting for transfers between devices, on_device(): gathered = lax.all_gather(blocks, ('y', 'core'), axis=0, tiled=True)  43.9 us
    ppermute x1, waiting for transfers between devices, on_device(): lax.ppermute(mine, 'z_hi', [(i, (i + 1) % halves) for i in range(halves)])  40.5 us
    all_to_all x1, blocking collectives, on_device(): got = lax.all_to_all(sent, 'x', 0, 0, tiled=True)  29.5 us
    dot_general x2, matrix products, on_device(): jnp.einsum('qdb,pqda->bpa', gathered[:, rows:], half, preferred_element_t...  19.4 us
    all_to_all x1, blocking collectives, on_device(): got = lax.all_to_all(summed, 'z_lo', 0, 0, tiled=True)  17.7 us
    ppermute x1, starting transfers between devices, on_device(): lax.ppermute(mine, 'z_hi', [(i, (i + 1) % halves) for i in range(halves)])  7.28 us
  transfers between devices with their start and end apart: 3, of which 3 were waited for; matrix products, arithmetic and copies ran while one was open for 5% of the time, Pallas kernels for 0%

profile of v5, /device:TPU:8, one launch (start us, length us, event | category | flops | bytes accessed | tf_op | source)
XLA Modules:
  0.0 186.7 jit_solution(16313840798447123909)
XLA Ops:
  6.5 0.0 copy-start
  6.5 0.0 all-gather.3.cloned.1.call-start
  6.5 0.8 copy.47
  7.4 0.8 copy.42
  8.2 1.3 copy.29
  9.5 0.3 mul.37
  9.8 1.1 mul.38
  10.9 1.4 multiply_convert_fusion
  12.2 1.0 copy.31
  13.2 0.1 fusion.19
  13.3 1.2 pad_maximum_fusion
  14.6 1.4 copy.32
  16.0 0.0 all-gather.3.cloned.1.call-update
  16.0 0.0 all-gather.5.cloned.1.call-start
  16.0 7.3 %collective-permute-start = (bf16[1,248,1920]{2,1,0:T(8,128)(2,1)}, bf16[1,248,1920]{2,1,0:T(8,128)(2,1)S(1)}, u32[]{:S(2)}, u32[]{:S(2)}) collective-permute-start(bf16[1,248,1920]{2,1,0:T(8,128)(2,1)} %copy.32), channel_id=1, source_target_pairs={{0,128},{128,0},{1,129},{129,1},{2,130},{130,2},{3,131},{131,3},{4... | collective-permute-start | bytes 2856968 | tf_op jit(solution)/shard_map/ppermute | solution.py:27
  23.3 40.5 %collective-permute-done = bf16[1,248,1920]{2,1,0:T(8,128)(2,1)S(1)} collective-permute-done((bf16[1,248,1920]{2,1,0:T(8,128)(2,1)}, bf16[1,248,1920]{2,1,0:T(8,128)(2,1)S(1)}, u32[]{:S(2)}, u32[]{:S(2)}) %collective-permute-start) | collective-permute-done | bytes 952352 | tf_op jit(solution)/shard_map/ppermute | solution.py:27
  63.8 0.0 copy-start.1
  63.9 0.9 copy-done.1
  64.8 0.0 all-gather.5.cloned.1.call-update
  64.8 2.3 %all-gather.3.cloned.1.call-done = bf16[8,248,1920]{2,1,0:T(8,128)(2,1)} async-done(((bf16[1,248,1920]{2,1,0:T(8,128)(2,1)}), bf16[8,248,1920]{2,1,0:T(8,128)(2,1)}) %all-gather.3.cloned.1.call-update) | async-done | bytes 7618576 | tf_op jit(solution)/shard_map/all_gather | solution.py:30
  67.2 0.0 copy-done
  67.2 9.4 %fusion.4 = f32[1920,4,128,1]{2,0,3,1:T(8,128)} fusion(bf16[8,248,1920]{2,1,0:T(8,128)(2,1)} %all-gather.3.cloned.1.call-done, bf16[4,120,1920]{2,1,0:T(8,128)(2,1)S(1)} %copy-done), kind=kOutput, calls=%fused_computation.9 | convolution fusion | flops 3775365120 | bytes 13393920 | tf_op jit(solution)/shard_map/qdb,pqda->bpa/dot_general | solution.py:34
  76.6 41.6 %all-gather.5.cloned.1.call-done = bf16[8,248,1920]{2,1,0:T(8,128)(2,1)} async-done(((bf16[1,248,1920]{2,1,0:T(8,128)(2,1)}), bf16[8,248,1920]{2,1,0:T(8,128)(2,1)}) %all-gather.5.cloned.1.call-update) | async-done | bytes 7618576 | tf_op jit(solution)/shard_map/all_gather | solution.py:30
  118.2 10.0 %fusion.2 = bf16[1920,4,128]{2,0,1:T(8,128)(2,1)} fusion(f32[1920,4,128,1]{2,0,3,1:T(8,128)} %fusion.4, bf16[8,248,1920]{2,1,0:T(8,128)(2,1)} %all-gather.5.cloned.1.call-done, bf16[4,120,1920]{2,1,0:T(8,128)(2,1)S(1)} %copy-done), kind=kOutput, calls=%fused_computation.5 | convolution fusion | flops 3777331200 | bytes 15360000 | tf_op jit(solution)/shard_map/qdb,pqda->bpa/dot_general | solution.py:34
  128.2 1.7 copy.34
  129.9 29.5 %all_to_all.10 = bf16[4,4,120,4,128]{4,2,1,3,0:T(8,128)(2,1)} all-to-all(bf16[4,4,120,4,128]{4,2,1,3,0:T(8,128)(2,1)S(1)} %copy.34), channel_id=1, replica_groups=mesh['z_hi'=2,'y'=4,'core'=2,'x'=4,'z_lo'=4] {'x'}, dimensions={0} | all-to-all | bytes 3932160 | tf_op jit(solution)/shard_map/all_to_all | solution.py:41
  159.4 1.9 %reduce_sum.21 = bf16[4,120,4,128]{3,1,0,2:T(8,128)(2,1)S(1)} reduce(bf16[4,4,120,4,128]{4,2,1,3,0:T(8,128)(2,1)} %all_to_all.10, bf16[]{:T(256)} %constant.2.clone.1), dimensions={0}, to_apply=%region_0.0 | reduce | flops 737280 | bytes 2457602 | tf_op jit(solution)/shard_map/reduce_sum | solution.py:42
  161.3 17.7 %all_to_all.11 = bf16[4,120,4,128]{3,1,2,0:T(8,128)(2,1)S(1)} all-to-all(bf16[4,120,4,128]{3,1,2,0:T(8,128)(2,1)S(1)} %copy.36), channel_id=1, replica_groups=mesh['z_hi'=2,'y'=4,'core'=2,'x'=4,'z_lo'=4] {'z_lo'}, dimensions={0} | all-to-all | bytes 983040 | tf_op jit(solution)/shard_map/all_to_all | solution.py:43
  179.0 0.1 convert_reduce_fusion
  179.1 0.8 copy.38
  (1 shorter events, 0.0 us)
Async XLA Ops:
  6.5 60.6 %copy-start = (bf16[4,120,1920]{2,1,0:T(8,128)(2,1)S(1)}, bf16[4,120,1920]{2,1,0:T(8,128)(2,1)}, u32[]{:S(2)}) copy-start(bf16[4,120,1920]{2,1,0:T(8,128)(2,1)} %param.9) | copy-start | bytes 5529604
  6.5 60.6 %all-gather.3.cloned.1.call-start = ((), (), s32[]{:S(2)}) async-start(), calls=%async_computation.2 | async-start | bytes 8570880 | tf_op jit(solution)/shard_map/all_gather | solution.py:30
  16.0 102.2 %all-gather.5.cloned.1.call-start = ((), (), s32[]{:S(2)}) async-start(), calls=%async_computation.3 | async-start | bytes 8570880 | tf_op jit(solution)/shard_map/all_gather | solution.py:30
  16.0 47.8 %collective-permute-start = (bf16[1,248,1920]{2,1,0:T(8,128)(2,1)}, bf16[1,248,1920]{2,1,0:T(8,128)(2,1)S(1)}, u32[]{:S(2)}, u32[]{:S(2)}) collective-permute-start(bf16[1,248,1920]{2,1,0:T(8,128)(2,1)} %copy.32), channel_id=1, source_target_pairs={{0,128},{128,0},{1,129},{129,1},{2,130},{130,2},{3,131},{131,3},{4... | collective-permute-start | bytes 2856968 | tf_op jit(solution)/shard_map/ppermute | solution.py:27
  63.8 0.9 copy-start.1
Sparse Core Ops, SparseCore 0:
  16.1 51.0 all-gather.2
  69.0 49.1 all-gather.4

commit v6 on v5

--- a/solution.py
+++ b/solution.py
@@ -18,6 +18,25 @@
     return wide.reshape(count, width, length).astype(jnp.bfloat16)
 
 
+def gather_y_core(blocks):
+    ring = lax.axis_size("y")
+    up = [(i, (i + 1) % ring) for i in range(ring)]
+    down = [(i, (i - 1) % ring) for i in range(ring)]
+    from_below = lax.ppermute(blocks, "y", up)
+    from_above = lax.ppermute(blocks, "y", down)
+    cut = blocks.shape[2] // 2
+    far = jnp.concatenate(
+        [
+            lax.ppermute(from_below[:, :, :cut], "y", up),
+            lax.ppermute(from_above[:, :, cut:], "y", down),
+        ],
+        axis=2,
+    )
+    chip = jnp.concatenate([blocks, from_below, far, from_above], axis=0)
+    other_core = lax.ppermute(chip, "core", [(0, 1), (1, 0)])
+    return jnp.concatenate([chip, other_core], axis=0)
+
+
 def on_device(row_codes, row_scales, panel_codes, panel_scales, amplitudes):
     row_local = decode_rows(row_codes, row_scales)
     panel_local = decode_rows(panel_codes, panel_scales)
@@ -27,7 +46,7 @@
     other = lax.ppermute(mine, "z_hi", [(i, (i + 1) % halves) for i in range(halves)])
     total = None
     for blocks in (mine, other):
-        gathered = lax.all_gather(blocks, ("y", "core"), axis=0, tiled=True)
+        gathered = gather_y_core(blocks)
         half = jnp.einsum(
             "qac,pdc->pqda", gathered[:, :rows], amplitudes, preferred_element_type=jnp.float32
         ).astype(jnp.bfloat16)

time: 188 us -> 183 us (0.973)
  waiting for transfers between devices: 84.5 us -> 60.5 us
  between operations: 13.4 us -> 0.14 us
  local copies, waits for them, and re-layouts: 10.2 us -> 20.5 us
  starting transfers between devices: 7.32 us -> 15.5 us
  blocking collectives: 47.1 us -> 54.7 us
  other arithmetic: 4.65 us -> 9.11 us
    all_gather x2 -> x0, waiting for transfers between devices: 43.9 us -> none  [on_device(): gathered = lax.all_gather(blocks, ('y', 'core'), axis=0, tiled=True)]
    ppermute x0 -> x10, waiting for transfers between devices: none -> 36.9 us  [the longest x2 27 us: gather_y_core(): from_above = lax.ppermute(blocks, 'y', down)]
    ppermute x1, waiting for transfers between devices: 40.5 us -> 23.6 us  [on_device(): lax.ppermute(mine, 'z_hi', [(i, (i + 1) % halves) for i in range(halves)])]
    ppermute x0 -> x10, starting transfers between devices: none -> 8.46 us  [the longest x2 3.88 us: gather_y_core(): from_above = lax.ppermute(blocks, 'y', down)]
    all_to_all x1, blocking collectives: 17.7 us -> 24.9 us  [on_device(): got = lax.all_to_all(summed, 'z_lo', 0, 0, tiled=True)]
    concatenate x1 -> x2, local copies, waits for them, and re-layouts: 1.39 us -> 6.42 us  [gather_y_core(): return jnp.concatenate([chip, other_core], axis=0)]
    unnamed x6 -> x12, local copies, waits for them, and re-layouts: 3.07 us -> 6.27 us
    concatenate x0 -> x2, other arithmetic: none -> 3.03 us  [gather_y_core(): chip = jnp.concatenate([blocks, from_below, far, from_above], axis=0)]
  transfers between devices with their start and end apart: 3 -> 11, of which waited for: 3 -> 6; matrix products, arithmetic and copies ran while one was open for 5% -> 11% of each run, Pallas kernels for 0% -> 0%
where the time goes in v6:
time: 183 us; the launch traced here: 180 us
  waiting for transfers between devices  60.5 us (33%)
  blocking collectives  54.7 us (30%)
  local copies, waits for them, and re-layouts  20.5 us (11%)
  matrix products  19.4 us (11%)
  starting transfers between devices  15.5 us (8%)
  other arithmetic  9.11 us (5%)
    all_to_all x1, blocking collectives, on_device(): got = lax.all_to_all(sent, 'x', 0, 0, tiled=True)  29.8 us
    ppermute x2, waiting for transfers between devices, gather_y_core(): from_above = lax.ppermute(blocks, 'y', down)  27 us
    all_to_all x1, blocking collectives, on_device(): got = lax.all_to_all(summed, 'z_lo', 0, 0, tiled=True)  24.9 us
    ppermute x1, waiting for transfers between devices, on_device(): lax.ppermute(mine, 'z_hi', [(i, (i + 1) % halves) for i in range(halves)])  23.6 us
    dot_general x2, matrix products, on_device(): jnp.einsum('qdb,pqda->bpa', gathered[:, rows:], half, preferred_element_t...  19.4 us
    ppermute x1, starting transfers between devices, on_device(): lax.ppermute(mine, 'z_hi', [(i, (i + 1) % halves) for i in range(halves)])  7.06 us
    ppermute x2, waiting for transfers between devices, gather_y_core(): lax.ppermute(from_above[:, :, cut:], 'y', down)  6.64 us
    concatenate x2, local copies, waits for them, and re-layouts, gather_y_core(): return jnp.concatenate([chip, other_core], axis=0)  6.42 us
  transfers between devices with their start and end apart: 11, of which 6 were waited for; matrix products, arithmetic and copies ran while one was open for 11% of the time, Pallas kernels for 0%

profile of v6, /device:TPU:8, one launch (start us, length us, event | category | flops | bytes accessed | tf_op | source)
XLA Modules:
  0.0 180.0 jit_solution(13941667018809879856)
XLA Ops:
  0.0 0.0 copy-start
  0.0 0.0 copy-start.1
  0.0 0.8 copy.29
  0.9 0.8 copy.24
  1.6 0.3 mul.37
  2.0 1.1 mul.38
  3.1 1.0 mul.33
  4.1 1.5 copy.14
  5.6 1.4 multiply_convert_fusion.1
  7.0 0.0 copy-done.1
  7.0 0.1 multiply_convert_fusion
  7.1 1.1 pad_maximum_fusion.3
  8.3 2.2 %collective-permute-start.2 = (bf16[1,248,1920]{2,1,0:T(8,128)(2,1)S(1)}, bf16[1,248,1920]{2,1,0:T(8,128)(2,1)S(1)}, u32[]{:S(2)}, u32[]{:S(2)}) collective-permute-start(bf16[1,248,1920]{2,1,0:T(8,128)(2,1)S(1)} %get-tuple-element.9), channel_id=1, source_target_pairs={{0,96},{32,0},{64,32},{96,64},{1,97},{33,1},{65,33},{97,65},{2,98}... | collective-permute-start | bytes 2856968 | tf_op jit(solution)/shard_map/ppermute | solution.py:26
  10.4 0.0 collective-permute-start
  10.4 7.1 %collective-permute-start.5 = (bf16[1,248,1920]{2,1,0:T(8,128)(2,1)S(1)}, bf16[1,248,1920]{2,1,0:T(8,128)(2,1)S(1)}, u32[]{:S(2)}, u32[]{:S(2)}) collective-permute-start(bf16[1,248,1920]{2,1,0:T(8,128)(2,1)S(1)} %get-tuple-element.9), channel_id=1, source_target_pairs={{0,128},{128,0},{1,129},{129,1},{2,130},{130,2},{3,131},{131,3},{4... | collective-permute-start | bytes 2856968 | tf_op jit(solution)/shard_map/ppermute | solution.py:46
  17.5 13.6 %collective-permute-done.2 = bf16[1,248,1920]{2,1,0:T(8,128)(2,1)S(1)} collective-permute-done((bf16[1,248,1920]{2,1,0:T(8,128)(2,1)S(1)}, bf16[1,248,1920]{2,1,0:T(8,128)(2,1)S(1)}, u32[]{:S(2)}, u32[]{:S(2)}) %collective-permute-start.2) | collective-permute-done | bytes 952352 | tf_op jit(solution)/shard_map/ppermute | solution.py:26
  31.1 0.2 slice.33
  31.3 1.1 collective-permute-start.3
  32.4 0.2 collective-permute-done
  32.6 0.1 slice.32
  32.6 1.0 collective-permute-start.1
  33.6 23.6 %collective-permute-done.5 = bf16[1,248,1920]{2,1,0:T(8,128)(2,1)S(1)} collective-permute-done((bf16[1,248,1920]{2,1,0:T(8,128)(2,1)S(1)}, bf16[1,248,1920]{2,1,0:T(8,128)(2,1)S(1)}, u32[]{:S(2)}, u32[]{:S(2)}) %collective-permute-start.5) | collective-permute-done | bytes 952352 | tf_op jit(solution)/shard_map/ppermute | solution.py:46
  57.2 1.7 collective-permute-start.8
  58.9 0.3 collective-permute-start.6
  59.2 1.1 constant_dynamic-update-slice_fusion.3
  60.3 0.0 collective-permute-done.3
  60.3 0.0 collective-permute-done.1
  60.3 1.2 constant_dynamic-update-slice_fusion.2
  61.5 0.8 pad_maximum_fusion
  62.3 0.1 collective-permute-start.4
  62.4 13.4 %collective-permute-done.8 = bf16[1,248,1920]{2,1,0:T(8,128)(2,1)S(1)} collective-permute-done((bf16[1,248,1920]{2,1,0:T(8,128)(2,1)S(1)}, bf16[1,248,1920]{2,1,0:T(8,128)(2,1)S(1)}, u32[]{:S(2)}, u32[]{:S(2)}) %collective-permute-start.8) | collective-permute-done | bytes 952352 | tf_op jit(solution)/shard_map/ppermute | solution.py:26
  75.8 0.2 slice.37
  76.0 1.4 collective-permute-start.9
  77.4 0.0 collective-permute-done.6
  77.4 0.8 collective-permute-start.7
  78.2 0.1 constant_dynamic-update-slice_fusion.9
  78.3 0.1 constant_dynamic-update-slice_fusion.8
  78.4 6.6 %collective-permute-done.9 = bf16[1,248,960]{2,1,0:T(8,128)(2,1)S(1)} collective-permute-done((bf16[1,248,960]{2,1,0:T(8,128)(2,1)S(1)}, bf16[1,248,960]{2,1,0:T(8,128)(2,1)S(1)}, u32[]{:S(2)}, u32[]{:S(2)}) %collective-permute-start.9) | collective-permute-done | bytes 476192 | tf_op jit(solution)/shard_map/ppermute | solution.py:31
  85.1 3.1 %collective-permute-done.7 = bf16[1,248,960]{2,1,0:T(8,128)(2,1)S(1)} collective-permute-done((bf16[1,248,960]{2,1,0:T(8,128)(2,1)S(1)}, bf16[1,248,960]{2,1,0:T(8,128)(2,1)S(1)}, u32[]{:S(2)}, u32[]{:S(2)}) %collective-permute-start.7) | collective-permute-done | bytes 476192 | tf_op jit(solution)/shard_map/ppermute | solution.py:30
  88.2 0.3 constant_dynamic-update-slice_fusion.7
  88.5 2.2 %pad_maximum_fusion.1 = bf16[4,248,1920]{2,1,0:T(8,128)(2,1)} fusion(bf16[1,248,1920]{2,1,0:T(8,128)(2,1)S(1)} %collective-permute-done.8, bf16[1,248,1920]{2,1,0:T(8,128)(2,1)S(1)} %get-tuple-element.6, bf16[1,248,1920]{2,1,0:T(8,128)(2,1)S(1)} %collective-permute-done.6, bf16[1,248,1920]{2,1,0:T(8,128)(2,1)S(1)} %collective-permute-done.5), kind=kLoop, calls=%fused_computation.7 | loop fusion | flops 5713920 | bytes 7618560 | tf_op jit(solution)/shard_map/concatenate | solution.py:35
  90.7 0.0 collective-permute-start.10
  90.8 1.0 constant_dynamic-update-slice_fusion.1
  91.8 0.1 constant_dynamic-update-slice_fusion.6
  91.9 0.0 copy-start.2
  91.9 0.0 collective-permute-done.4
  91.9 3.0 %copy-done.2 = bf16[8,248,1920]{2,1,0:T(8,128)(2,1)} copy-done((bf16[8,248,1920]{2,1,0:T(8,128)(2,1)}, bf16[8,248,1920]{2,1,0:T(8,128)(2,1)S(1)}, u32[]{:S(2)}) %copy-start.2) | copy-done | bytes 7618584
  94.9 2.2 %constant_dynamic-update-slice_fusion = bf16[8,248,1920]{2,1,0:T(8,128)(2,1)} fusion(bf16[8,248,1920]{2,1,0:T(8,128)(2,1)} %constant_dynamic-update-slice_fusion.1, bf16[4,248,1920]{2,1,0:T(8,128)(2,1)S(1)} %collective-permute-done.4), kind=kLoop, calls=%fused_computation.24 | loop fusion | bytes 7618560 | tf_op jit(solution)/shard_map/concatenate | solution.py:37
  97.1 0.0 copy-done
  97.1 9.4 %fusion.4 = f32[1920,4,128,1]{2,0,3,1:T(8,128)} fusion(bf16[8,248,1920]{2,1,0:T(8,128)(2,1)} %constant_dynamic-update-slice_fusion, bf16[4,120,1920]{2,1,0:T(8,128)(2,1)S(1)} %copy-done), kind=kOutput, calls=%fused_computation.11 | convolution fusion | flops 3775365120 | bytes 13393920 | tf_op jit(solution)/shard_map/qdb,pqda->bpa/dot_general | solution.py:53
  106.5 0.0 collective-permute-done.10
  106.5 4.2 %constant_dynamic-update-slice_fusion.5 = bf16[8,248,1920]{2,1,0:T(8,128)(2,1)} fusion(bf16[8,248,1920]{2,1,0:T(8,128)(2,1)} %copy-done.2, bf16[4,248,1920]{2,1,0:T(8,128)(2,1)} %collective-permute-done.10), kind=kLoop, calls=%fused_computation.29 | loop fusion | bytes 7618560 | tf_op jit(solution)/shard_map/concatenate | solution.py:37
  110.8 10.0 %fusion.2 = bf16[1920,4,128]{2,0,1:T(8,128)(2,1)} fusion(f32[1920,4,128,1]{2,0,3,1:T(8,128)} %fusion.4, bf16[8,248,1920]{2,1,0:T(8,128)(2,1)} %constant_dynamic-update-slice_fusion.5, bf16[4,120,1920]{2,1,0:T(8,128)(2,1)S(1)} %copy-done), kind=kOutput, calls=%fused_computation.5 | convolution fusion | flops 3777331200 | bytes 15360000 | tf_op jit(solution)/shard_map/qdb,pqda->bpa/dot_general | solution.py:53
  120.8 1.7 copy.16
  122.5 29.8 %all_to_all.10 = bf16[4,4,120,4,128]{4,2,1,3,0:T(8,128)(2,1)} all-to-all(bf16[4,4,120,4,128]{4,2,1,3,0:T(8,128)(2,1)S(1)} %copy.16), channel_id=1, replica_groups=mesh['z_hi'=2,'y'=4,'core'=2,'x'=4,'z_lo'=4] {'x'}, dimensions={0} | all-to-all | bytes 3932160 | tf_op jit(solution)/shard_map/all_to_all | solution.py:60
  152.3 1.9 %reduce_sum.21 = bf16[4,120,4,128]{3,1,0,2:T(8,128)(2,1)S(1)} reduce(bf16[4,4,120,4,128]{4,2,1,3,0:T(8,128)(2,1)} %all_to_all.10, bf16[]{:T(256)} %constant.2.clone.1), dimensions={0}, to_apply=%region_0.0 | reduce | flops 737280 | bytes 2457602 | tf_op jit(solution)/shard_map/reduce_sum | solution.py:61
  154.2 24.9 %all_to_all.11 = bf16[4,120,4,128]{3,1,2,0:T(8,128)(2,1)S(1)} all-to-all(bf16[4,120,4,128]{3,1,2,0:T(8,128)(2,1)S(1)} %copy.18), channel_id=1, replica_groups=mesh['z_hi'=2,'y'=4,'core'=2,'x'=4,'z_lo'=4] {'z_lo'}, dimensions={0} | all-to-all | bytes 983040 | tf_op jit(solution)/shard_map/all_to_all | solution.py:62
  179.2 0.1 convert_reduce_fusion
  179.2 0.8 copy.20
  (2 shorter events, 0.1 us)
Async XLA Ops:
  0.0 97.1 %copy-start = (bf16[4,120,1920]{2,1,0:T(8,128)(2,1)S(1)}, bf16[4,120,1920]{2,1,0:T(8,128)(2,1)}, u32[]{:S(2)}) copy-start(bf16[4,120,1920]{2,1,0:T(8,128)(2,1)} %param.9) | copy-start | bytes 5529604
  0.0 7.0 %copy-start.1 = (bf16[1,128,1920]{2,1,0:T(8,128)(2,1)S(1)}, bf16[1,128,1920]{2,1,0:T(8,128)(2,1)}, u32[]{:S(2)}) copy-start(bf16[1,128,1920]{2,1,0:T(8,128)(2,1)} %param.5) | copy-start | bytes 1474564
  8.3 22.8 %collective-permute-start.2 = (bf16[1,248,1920]{2,1,0:T(8,128)(2,1)S(1)}, bf16[1,248,1920]{2,1,0:T(8,128)(2,1)S(1)}, u32[]{:S(2)}, u32[]{:S(2)}) collective-permute-start(bf16[1,248,1920]{2,1,0:T(8,128)(2,1)S(1)} %get-tuple-element.9), channel_id=1, source_target_pairs={{0,96},{32,0},{64,32},{96,64},{1,97},{33,1},{65,33},{97,65},{2,98}... | collective-permute-start | bytes 2856968 | tf_op jit(solution)/shard_map/ppermute | solution.py:26
  10.4 22.1 %collective-permute-start = (bf16[1,248,1920]{2,1,0:T(8,128)(2,1)S(1)}, bf16[1,248,1920]{2,1,0:T(8,128)(2,1)S(1)}, u32[]{:S(2)}, u32[]{:S(2)}) collective-permute-start(bf16[1,248,1920]{2,1,0:T(8,128)(2,1)S(1)} %get-tuple-element.9), channel_id=1, source_target_pairs={{0,32},{32,64},{64,96},{96,0},{1,33},{33,65},{65,97},{97,1},{2,34}... | collective-permute-start | bytes 2856968 | tf_op jit(solution)/shard_map/ppermute | solution.py:25
  10.4 46.7 %collective-permute-start.5 = (bf16[1,248,1920]{2,1,0:T(8,128)(2,1)S(1)}, bf16[1,248,1920]{2,1,0:T(8,128)(2,1)S(1)}, u32[]{:S(2)}, u32[]{:S(2)}) collective-permute-start(bf16[1,248,1920]{2,1,0:T(8,128)(2,1)S(1)} %get-tuple-element.9), channel_id=1, source_target_pairs={{0,128},{128,0},{1,129},{129,1},{2,130},{130,2},{3,131},{131,3},{4... | collective-permute-start | bytes 2856968 | tf_op jit(solution)/shard_map/ppermute | solution.py:46
  31.3 29.0 %collective-permute-start.3 = (bf16[1,248,960]{2,1,0:T(8,128)(2,1)S(1)}, bf16[1,248,960]{2,1,0:T(8,128)(2,1)S(1)}, u32[]{:S(2)}, u32[]{:S(2)}) collective-permute-start(bf16[1,248,960]{2,1,0:T(8,128)(2,1)S(1)} %slice.33), channel_id=1, source_target_pairs={{0,96},{32,0},{64,32},{96,64},{1,97},{33,1},{65,33},{97,65},{2,98}... | collective-permute-start | bytes 1428488 | tf_op jit(solution)/shard_map/ppermute | solution.py:31
  32.6 27.7 %collective-permute-start.1 = (bf16[1,248,960]{2,1,0:T(8,128)(2,1)S(1)}, bf16[1,248,960]{2,1,0:T(8,128)(2,1)S(1)}, u32[]{:S(2)}, u32[]{:S(2)}) collective-permute-start(bf16[1,248,960]{2,1,0:T(8,128)(2,1)S(1)} %slice.32), channel_id=1, source_target_pairs={{0,32},{32,64},{64,96},{96,0},{1,33},{33,65},{65,97},{97,1},{2,34}... | collective-permute-start | bytes 1428488 | tf_op jit(solution)/shard_map/ppermute | solution.py:30
  57.2 18.6 %collective-permute-start.8 = (bf16[1,248,1920]{2,1,0:T(8,128)(2,1)S(1)}, bf16[1,248,1920]{2,1,0:T(8,128)(2,1)S(1)}, u32[]{:S(2)}, u32[]{:S(2)}) collective-permute-start(bf16[1,248,1920]{2,1,0:T(8,128)(2,1)S(1)} %collective-permute-done.5), channel_id=1, source_target_pairs={{0,96},{32,0},{64,32},{96,64},{1,97},{33,1},{65,33},{97,65},{2,98}... | collective-permute-start | bytes 2856968 | tf_op jit(solution)/shard_map/ppermute | solution.py:26
  58.9 18.5 %collective-permute-start.6 = (bf16[1,248,1920]{2,1,0:T(8,128)(2,1)S(1)}, bf16[1,248,1920]{2,1,0:T(8,128)(2,1)S(1)}, u32[]{:S(2)}, u32[]{:S(2)}) collective-permute-start(bf16[1,248,1920]{2,1,0:T(8,128)(2,1)S(1)} %collective-permute-done.5), channel_id=1, source_target_pairs={{0,32},{32,64},{64,96},{96,0},{1,33},{33,65},{65,97},{97,1},{2,34}... | collective-permute-start | bytes 2856968 | tf_op jit(solution)/shard_map/ppermute | solution.py:25
  62.3 29.6 %collective-permute-start.4 = (bf16[4,248,1920]{2,1,0:T(8,128)(2,1)S(1)}, bf16[4,248,1920]{2,1,0:T(8,128)(2,1)S(1)}, u32[]{:S(2)}, u32[]{:S(2)}) collective-permute-start(bf16[4,248,1920]{2,1,0:T(8,128)(2,1)S(1)} %pad_maximum_fusion), channel_id=1, source_target_pairs={{0,16},{16,0},{1,17},{17,1},{2,18},{18,2},{3,19},{19,3},{4,20},{20... | collective-permute-start | bytes 11427848 | tf_op jit(solution)/shard_map/ppermute | solution.py:36
  76.0 9.1 %collective-permute-start.9 = (bf16[1,248,960]{2,1,0:T(8,128)(2,1)S(1)}, bf16[1,248,960]{2,1,0:T(8,128)(2,1)S(1)}, u32[]{:S(2)}, u32[]{:S(2)}) collective-permute-start(bf16[1,248,960]{2,1,0:T(8,128)(2,1)S(1)} %slice.37), channel_id=1, source_target_pairs={{0,96},{32,0},{64,32},{96,64},{1,97},{33,1},{65,33},{97,65},{2,98}... | collective-permute-start | bytes 1428488 | tf_op jit(solution)/shard_map/ppermute | solution.py:31
  77.4 10.7 %collective-permute-start.7 = (bf16[1,248,960]{2,1,0:T(8,128)(2,1)S(1)}, bf16[1,248,960]{2,1,0:T(8,128)(2,1)S(1)}, u32[]{:S(2)}, u32[]{:S(2)}) collective-permute-start(bf16[1,248,960]{2,1,0:T(8,128)(2,1)S(1)} %slice.36), channel_id=1, source_target_pairs={{0,32},{32,64},{64,96},{96,0},{1,33},{33,65},{65,97},{97,1},{2,34}... | collective-permute-start | bytes 1428488 | tf_op jit(solution)/shard_map/ppermute | solution.py:30
  90.7 15.8 %collective-permute-start.10 = (bf16[4,248,1920]{2,1,0:T(8,128)(2,1)}, bf16[4,248,1920]{2,1,0:T(8,128)(2,1)}, u32[]{:S(2)}, u32[]{:S(2)}) collective-permute-start(bf16[4,248,1920]{2,1,0:T(8,128)(2,1)} %pad_maximum_fusion.1), channel_id=1, source_target_pairs={{0,16},{16,0},{1,17},{17,1},{2,18},{18,2},{3,19},{19,3},{4,20},{20... | collective-permute-start | bytes 11427848 | tf_op jit(solution)/shard_map/ppermute | solution.py:36
  91.9 3.0 %copy-start.2 = (bf16[8,248,1920]{2,1,0:T(8,128)(2,1)}, bf16[8,248,1920]{2,1,0:T(8,128)(2,1)S(1)}, u32[]{:S(2)}) copy-start(bf16[8,248,1920]{2,1,0:T(8,128)(2,1)S(1)} %constant_dynamic-update-slice_fusion.6) | copy-start | bytes 22855684

commit v7 on v6

--- a/solution.py
+++ b/solution.py
@@ -18,12 +18,14 @@
     return wide.reshape(count, width, length).astype(jnp.bfloat16)
 
 
-def gather_y_core(blocks):
+def gather_y_core(blocks, after):
     ring = lax.axis_size("y")
     up = [(i, (i + 1) % ring) for i in range(ring)]
     down = [(i, (i - 1) % ring) for i in range(ring)]
     from_below = lax.ppermute(blocks, "y", up)
     from_above = lax.ppermute(blocks, "y", down)
+    if after is not None:
+        after, from_below, from_above = lax.optimization_barrier((after, from_below, from_above))
     cut = blocks.shape[2] // 2
     far = jnp.concatenate(
         [
@@ -34,10 +36,10 @@
     )
     chip = jnp.concatenate([blocks, from_below, far, from_above], axis=0)
     other_core = lax.ppermute(chip, "core", [(0, 1), (1, 0)])
-    return jnp.concatenate([chip, other_core], axis=0)
+    return jnp.concatenate([chip, other_core], axis=0), after
 
 
-def on_device(row_codes, row_scales, panel_codes, panel_scales, amplitudes):
+def ladder(row_codes, row_scales, panel_codes, panel_scales, amplitudes):
     row_local = decode_rows(row_codes, row_scales)
     panel_local = decode_rows(panel_codes, panel_scales)
     rows = row_local.shape[1]
@@ -46,7 +48,7 @@
     other = lax.ppermute(mine, "z_hi", [(i, (i + 1) % halves) for i in range(halves)])
     total = None
     for blocks in (mine, other):
-        gathered = gather_y_core(blocks)
+        gathered, total = gather_y_core(blocks, total)
         half = jnp.einsum(
             "qac,pdc->pqda", gathered[:, :rows], amplitudes, preferred_element_type=jnp.float32
         ).astype(jnp.bfloat16)
@@ -62,6 +64,7 @@
     got = lax.all_to_all(summed, "z_lo", 0, 0, tiled=True)
     return got.astype(jnp.float32).sum(axis=0)
 
+
 def solution(mesh):
     sizes = dict(z_hi=2, y=4, core=2, x=4, z_lo=4)
     fine = Mesh(mesh.devices.reshape([sizes[n] for n in AUX + VIRT]), AUX + VIRT)
@@ -73,5 +76,5 @@
         P(AUX, VIRT, None),
     )
     return jax.shard_map(
-        on_device, mesh=fine, in_specs=placed, out_specs=P(VIRT, AUX, None), check_vma=False
+        ladder, mesh=fine, in_specs=placed, out_specs=P(VIRT, AUX, None), check_vma=False
     )

time: 183 us -> 213 us (1.16)
  waiting for transfers between devices: 60.5 us -> 90 us
  other arithmetic: 9.11 us -> 13.3 us
  blocking collectives: 54.7 us -> 52 us
    ppermute x1, waiting for transfers between devices: 23.6 us -> 40.8 us  [ladder(): lax.ppermute(mine, 'z_hi', [(i, (i + 1) % halves) for i in range(halves)])]
    ppermute x2, waiting for transfers between devices: 0.01 us -> 5.6 us  [gather_y_core(): other_core = lax.ppermute(chip, 'core', [(0, 1), (1, 0)])]
    ppermute x2, waiting for transfers between devices: 6.64 us -> 11.7 us  [gather_y_core(): lax.ppermute(from_above[:, :, cut:], 'y', down)]
    convert_element_type x0 -> x1, other arithmetic: none -> 3.69 us  [ladder(): total.astype(jnp.bfloat16).reshape(across, along, width, *total.shape[1:])]
    all_to_all x2, blocking collectives: 54.7 us -> 52 us  [the longest x1 29.4 us: ladder(): got = lax.all_to_all(sent, 'x', 0, 0, tiled=True)]
    ppermute x2, waiting for transfers between devices: 0.18 us -> 2.36 us  [gather_y_core(): from_below = lax.ppermute(blocks, 'y', up)]
    concatenate x2, local copies, waits for them, and re-layouts: 6.42 us -> 4.27 us  [gather_y_core(): return (jnp.concatenate([chip, other_core], axis=0), after)]
    unnamed x12 -> x10, local copies, waits for them, and re-layouts: 6.27 us -> 8.41 us
  transfers between devices with their start and end apart: 11 -> 11, of which waited for: 6 -> 10; matrix products, arithmetic and copies ran while one was open for 11% -> 9% of each run, Pallas kernels for 0% -> 0%
where the time goes in v7:
time: 213 us; the launch traced here: 211 us
  waiting for transfers between devices  90 us (42%)
  blocking collectives  52 us (24%)
  local copies, waits for them, and re-layouts  20 us (9%)
  matrix products  19 us (9%)
  starting transfers between devices  16.9 us (8%)
  other arithmetic  13.3 us (6%)
    ppermute x1, waiting for transfers between devices, ladder(): lax.ppermute(mine, 'z_hi', [(i, (i + 1) % halves) for i in range(halves)])  40.8 us
    all_to_all x1, blocking collectives, ladder(): got = lax.all_to_all(sent, 'x', 0, 0, tiled=True)  29.4 us
    ppermute x2, waiting for transfers between devices, gather_y_core(): from_above = lax.ppermute(blocks, 'y', down)  25 us
    all_to_all x1, blocking collectives, ladder(): got = lax.all_to_all(summed, 'z_lo', 0, 0, tiled=True)  22.6 us
    dot_general x2, matrix products, ladder(): jnp.einsum('qdb,pqda->bpa', gathered[:, rows:], half, preferred_element_t...  19 us
    ppermute x2, waiting for transfers between devices, gather_y_core(): lax.ppermute(from_above[:, :, cut:], 'y', down)  11.7 us
    unnamed x10, local copies, waits for them, and re-layouts  8.41 us
    ppermute x1, starting transfers between devices, ladder(): lax.ppermute(mine, 'z_hi', [(i, (i + 1) % halves) for i in range(halves)])  7.28 us
  transfers between devices with their start and end apart: 11, of which 10 were waited for; matrix products, arithmetic and copies ran while one was open for 9% of the time, Pallas kernels for 0%

profile of v7, /device:TPU:8, one launch (start us, length us, event | category | flops | bytes accessed | tf_op | source)
XLA Modules:
  0.0 211.4 jit_solution(10645708045159796133)
XLA Ops:
  0.0 0.0 copy-start
  0.0 0.0 copy-start.1
  0.0 0.8 copy.29
  0.9 0.8 copy.24
  1.6 0.3 mul.37
  2.0 1.1 mul.38
  3.1 1.0 mul.33
  4.1 1.5 copy.14
  5.7 1.4 multiply_convert_fusion.1
  7.0 0.0 copy-done.1
  7.1 0.1 multiply_convert_fusion
  7.1 1.1 pad_maximum_fusion.3
  8.2 2.2 %collective-permute-start.2 = (bf16[1,248,1920]{2,1,0:T(8,128)(2,1)S(1)}, bf16[1,248,1920]{2,1,0:T(8,128)(2,1)S(1)}, u32[]{:S(2)}, u32[]{:S(2)}) collective-permute-start(bf16[1,248,1920]{2,1,0:T(8,128)(2,1)S(1)} %get-tuple-element.15), channel_id=1, source_target_pairs={{0,96},{32,0},{64,32},{96,64},{1,97},{33,1},{65,33},{97,65},{2,98}... | collective-permute-start | bytes 2856968 | tf_op jit(solution)/shard_map/ppermute | solution.py:26
  10.4 0.0 collective-permute-start
  10.4 20.7 %collective-permute-done.2 = bf16[1,248,1920]{2,1,0:T(8,128)(2,1)S(1)} collective-permute-done((bf16[1,248,1920]{2,1,0:T(8,128)(2,1)S(1)}, bf16[1,248,1920]{2,1,0:T(8,128)(2,1)S(1)}, u32[]{:S(2)}, u32[]{:S(2)}) %collective-permute-start.2) | collective-permute-done | bytes 952352 | tf_op jit(solution)/shard_map/ppermute | solution.py:26
  31.1 0.2 slice.33
  31.3 1.1 collective-permute-start.3
  32.3 0.2 collective-permute-done
  32.5 0.1 slice.32
  32.6 1.0 collective-permute-start.1
  33.5 1.1 constant_dynamic-update-slice_fusion.3
  34.6 9.2 %collective-permute-done.3 = bf16[1,248,960]{2,1,0:T(8,128)(2,1)S(1)} collective-permute-done((bf16[1,248,960]{2,1,0:T(8,128)(2,1)S(1)}, bf16[1,248,960]{2,1,0:T(8,128)(2,1)S(1)}, u32[]{:S(2)}, u32[]{:S(2)}) %collective-permute-start.3) | collective-permute-done | bytes 476192 | tf_op jit(solution)/shard_map/ppermute | solution.py:33
  43.8 2.8 %collective-permute-done.1 = bf16[1,248,960]{2,1,0:T(8,128)(2,1)S(1)} collective-permute-done((bf16[1,248,960]{2,1,0:T(8,128)(2,1)S(1)}, bf16[1,248,960]{2,1,0:T(8,128)(2,1)S(1)}, u32[]{:S(2)}, u32[]{:S(2)}) %collective-permute-start.1) | collective-permute-done | bytes 476192 | tf_op jit(solution)/shard_map/ppermute | solution.py:32
  46.6 1.2 constant_dynamic-update-slice_fusion.2
  47.9 0.8 pad_maximum_fusion
  48.6 0.1 collective-permute-start.4
  48.7 7.3 %collective-permute-start.5 = (bf16[1,248,1920]{2,1,0:T(8,128)(2,1)S(1)}, bf16[1,248,1920]{2,1,0:T(8,128)(2,1)}, u32[]{:S(2)}, u32[]{:S(2)}) collective-permute-start(bf16[1,248,1920]{2,1,0:T(8,128)(2,1)S(1)} %get-tuple-element.15), channel_id=1, source_target_pairs={{0,128},{128,0},{1,129},{129,1},{2,130},{130,2},{3,131},{131,3},{4... | collective-permute-start | bytes 2856968 | tf_op jit(solution)/shard_map/ppermute | solution.py:48
  56.0 40.8 %collective-permute-done.5 = bf16[1,248,1920]{2,1,0:T(8,128)(2,1)} collective-permute-done((bf16[1,248,1920]{2,1,0:T(8,128)(2,1)S(1)}, bf16[1,248,1920]{2,1,0:T(8,128)(2,1)}, u32[]{:S(2)}, u32[]{:S(2)}) %collective-permute-start.5) | collective-permute-done | bytes 952352 | tf_op jit(solution)/shard_map/ppermute | solution.py:48
  96.8 3.0 %collective-permute-start.7 = (bf16[1,248,1920]{2,1,0:T(8,128)(2,1)}, bf16[1,248,1920]{2,1,0:T(8,128)(2,1)S(1)}, u32[]{:S(2)}, u32[]{:S(2)}) collective-permute-start(bf16[1,248,1920]{2,1,0:T(8,128)(2,1)} %collective-permute-done.5), channel_id=1, source_target_pairs={{0,96},{32,0},{64,32},{96,64},{1,97},{33,1},{65,33},{97,65},{2,98}... | collective-permute-start | bytes 2856968 | tf_op jit(solution)/shard_map/ppermute | solution.py:26
  99.8 0.0 collective-permute-start.6
  99.8 1.0 constant_dynamic-update-slice_fusion.1
  100.8 0.0 collective-permute-done.4
  100.8 2.1 %constant_dynamic-update-slice_fusion = bf16[8,248,1920]{2,1,0:T(8,128)(2,1)} fusion(bf16[8,248,1920]{2,1,0:T(8,128)(2,1)} %constant_dynamic-update-slice_fusion.1, bf16[4,248,1920]{2,1,0:T(8,128)(2,1)S(1)} %collective-permute-done.4), kind=kLoop, calls=%fused_computation.25 | loop fusion | bytes 7618560 | tf_op jit(solution)/shard_map/concatenate | solution.py:39
  102.9 0.0 copy-done
  102.9 9.5 %fusion.5 = f32[1920,4,128]{2,0,1:T(8,128)} fusion(bf16[8,248,1920]{2,1,0:T(8,128)(2,1)} %constant_dynamic-update-slice_fusion, bf16[4,120,1920]{2,1,0:T(8,128)(2,1)S(1)} %copy-done), kind=kOutput, calls=%fused_computation.12 | convolution fusion | flops 3775365120 | bytes 13393920 | tf_op jit(solution)/shard_map/qdb,pqda->bpa/dot_general | solution.py:55
  112.4 4.3 %collective-permute-done.7 = bf16[1,248,1920]{2,1,0:T(8,128)(2,1)S(1)} collective-permute-done((bf16[1,248,1920]{2,1,0:T(8,128)(2,1)}, bf16[1,248,1920]{2,1,0:T(8,128)(2,1)S(1)}, u32[]{:S(2)}, u32[]{:S(2)}) %collective-permute-start.7) | collective-permute-done | bytes 952352 | tf_op jit(solution)/shard_map/ppermute | solution.py:26
  116.8 2.2 %collective-permute-done.6 = bf16[1,248,1920]{2,1,0:T(8,128)(2,1)} collective-permute-done((bf16[1,248,1920]{2,1,0:T(8,128)(2,1)}, bf16[1,248,1920]{2,1,0:T(8,128)(2,1)}, u32[]{:S(2)}, u32[]{:S(2)}) %collective-permute-start.6) | collective-permute-done | bytes 952352 | tf_op jit(solution)/shard_map/ppermute | solution.py:25
  119.0 1.1 slice.28
  120.1 0.2 slice.29
  120.3 1.9 collective-permute-start.9
  122.2 0.4 collective-permute-start.8
  122.6 2.2 %constant_dynamic-update-slice_fusion.9 = bf16[8,248,1920]{2,1,0:T(8,128)(2,1)} fusion(bf16[1,248,1920]{2,1,0:T(8,128)(2,1)} %collective-permute-done.5), kind=kLoop, calls=%fused_computation.34 | loop fusion | bytes 1904640
  124.8 2.3 %constant_dynamic-update-slice_fusion.8 = bf16[8,248,1920]{2,1,0:T(8,128)(2,1)} fusion(bf16[8,248,1920]{2,1,0:T(8,128)(2,1)} %constant_dynamic-update-slice_fusion.9, bf16[1,248,1920]{2,1,0:T(8,128)(2,1)} %collective-permute-done.6), kind=kLoop, calls=%fused_computation.33 | loop fusion | bytes 1904640
  127.0 2.5 %collective-permute-done.9 = bf16[1,248,960]{2,1,0:T(8,128)(2,1)S(1)} collective-permute-done((bf16[1,248,960]{2,1,0:T(8,128)(2,1)S(1)}, bf16[1,248,960]{2,1,0:T(8,128)(2,1)S(1)}, u32[]{:S(2)}, u32[]{:S(2)}) %collective-permute-start.9) | collective-permute-done | bytes 476192 | tf_op jit(solution)/shard_map/ppermute | solution.py:33
  129.5 1.7 collective-permute-done.8
  131.2 1.2 constant_dynamic-update-slice_fusion.7
  132.4 1.9 pad_maximum_fusion.1
  134.3 0.1 collective-permute-start.10
  134.4 1.0 constant_dynamic-update-slice_fusion.6
  135.4 5.6 %collective-permute-done.10 = bf16[4,248,1920]{2,1,0:T(8,128)(2,1)S(1)} collective-permute-done((bf16[4,248,1920]{2,1,0:T(8,128)(2,1)S(1)}, bf16[4,248,1920]{2,1,0:T(8,128)(2,1)S(1)}, u32[]{:S(2)}, u32[]{:S(2)}) %collective-permute-start.10) | collective-permute-done | bytes 3809312 | tf_op jit(solution)/shard_map/ppermute | solution.py:38
  141.0 2.1 %constant_dynamic-update-slice_fusion.5 = bf16[8,248,1920]{2,1,0:T(8,128)(2,1)} fusion(bf16[8,248,1920]{2,1,0:T(8,128)(2,1)} %constant_dynamic-update-slice_fusion.6, bf16[4,248,1920]{2,1,0:T(8,128)(2,1)S(1)} %collective-permute-done.10), kind=kLoop, calls=%fused_computation.30 | loop fusion | bytes 7618560 | tf_op jit(solution)/shard_map/concatenate | solution.py:39
  143.2 9.5 %fusion.3 = f32[1920,4,128,1]{2,0,3,1:T(8,128)} fusion(bf16[8,248,1920]{2,1,0:T(8,128)(2,1)} %constant_dynamic-update-slice_fusion.5, bf16[4,120,1920]{2,1,0:T(8,128)(2,1)S(1)} %copy-done), kind=kOutput, calls=%fused_computation.9 | convolution fusion | flops 3775365120 | bytes 13393920 | tf_op jit(solution)/shard_map/qdb,pqda->bpa/dot_general | solution.py:55
  152.7 3.7 %fusion.2 = bf16[1920,4,128]{2,0,1:T(8,128)(2,1)S(1)} fusion(f32[1920,4,128]{2,0,1:T(8,128)} %fusion.5, f32[1920,4,128,1]{2,0,3,1:T(8,128)} %fusion.3), kind=kLoop, calls=%fused_computation.5 | loop fusion | flops 1966080 | bytes 9830400 | tf_op jit(solution)/shard_map/convert_element_type | solution.py:61
  156.4 0.2 copy.16
  156.6 29.4 %all_to_all.10 = bf16[4,4,120,4,128]{4,2,1,3,0:T(8,128)(2,1)} all-to-all(bf16[4,4,120,4,128]{4,2,1,3,0:T(8,128)(2,1)S(1)} %copy.16), channel_id=1, replica_groups=mesh['z_hi'=2,'y'=4,'core'=2,'x'=4,'z_lo'=4] {'x'}, dimensions={0} | all-to-all | bytes 3932160 | tf_op jit(solution)/shard_map/all_to_all | solution.py:62
  186.0 1.9 reduce_sum.21
  187.9 22.6 %all_to_all.11 = bf16[4,120,4,128]{3,1,2,0:T(8,128)(2,1)S(1)} all-to-all(bf16[4,120,4,128]{3,1,2,0:T(8,128)(2,1)S(1)} %copy.18), channel_id=1, replica_groups=mesh['z_hi'=2,'y'=4,'core'=2,'x'=4,'z_lo'=4] {'z_lo'}, dimensions={0} | all-to-all | bytes 983040 | tf_op jit(solution)/shard_map/all_to_all | solution.py:64
  210.5 0.1 convert_reduce_fusion
  210.6 0.8 copy.20
  (1 shorter events, 0.0 us)
Async XLA Ops:
  0.0 102.9 %copy-start = (bf16[4,120,1920]{2,1,0:T(8,128)(2,1)S(1)}, bf16[4,120,1920]{2,1,0:T(8,128)(2,1)}, u32[]{:S(2)}) copy-start(bf16[4,120,1920]{2,1,0:T(8,128)(2,1)} %param.9) | copy-start | bytes 5529604
  0.0 7.0 %copy-start.1 = (bf16[1,128,1920]{2,1,0:T(8,128)(2,1)S(1)}, bf16[1,128,1920]{2,1,0:T(8,128)(2,1)}, u32[]{:S(2)}) copy-start(bf16[1,128,1920]{2,1,0:T(8,128)(2,1)} %param.5) | copy-start | bytes 1474564
  8.2 22.8 %collective-permute-start.2 = (bf16[1,248,1920]{2,1,0:T(8,128)(2,1)S(1)}, bf16[1,248,1920]{2,1,0:T(8,128)(2,1)S(1)}, u32[]{:S(2)}, u32[]{:S(2)}) collective-permute-start(bf16[1,248,1920]{2,1,0:T(8,128)(2,1)S(1)} %get-tuple-element.15), channel_id=1, source_target_pairs={{0,96},{32,0},{64,32},{96,64},{1,97},{33,1},{65,33},{97,65},{2,98}... | collective-permute-start | bytes 2856968 | tf_op jit(solution)/shard_map/ppermute | solution.py:26
  10.4 22.1 %collective-permute-start = (bf16[1,248,1920]{2,1,0:T(8,128)(2,1)S(1)}, bf16[1,248,1920]{2,1,0:T(8,128)(2,1)S(1)}, u32[]{:S(2)}, u32[]{:S(2)}) collective-permute-start(bf16[1,248,1920]{2,1,0:T(8,128)(2,1)S(1)} %get-tuple-element.15), channel_id=1, source_target_pairs={{0,32},{32,64},{64,96},{96,0},{1,33},{33,65},{65,97},{97,1},{2,34}... | collective-permute-start | bytes 2856968 | tf_op jit(solution)/shard_map/ppermute | solution.py:25
  31.3 12.5 %collective-permute-start.3 = (bf16[1,248,960]{2,1,0:T(8,128)(2,1)S(1)}, bf16[1,248,960]{2,1,0:T(8,128)(2,1)S(1)}, u32[]{:S(2)}, u32[]{:S(2)}) collective-permute-start(bf16[1,248,960]{2,1,0:T(8,128)(2,1)S(1)} %slice.33), channel_id=1, source_target_pairs={{0,96},{32,0},{64,32},{96,64},{1,97},{33,1},{65,33},{97,65},{2,98}... | collective-permute-start | bytes 1428488 | tf_op jit(solution)/shard_map/ppermute | solution.py:33
  32.6 14.0 %collective-permute-start.1 = (bf16[1,248,960]{2,1,0:T(8,128)(2,1)S(1)}, bf16[1,248,960]{2,1,0:T(8,128)(2,1)S(1)}, u32[]{:S(2)}, u32[]{:S(2)}) collective-permute-start(bf16[1,248,960]{2,1,0:T(8,128)(2,1)S(1)} %slice.32), channel_id=1, source_target_pairs={{0,32},{32,64},{64,96},{96,0},{1,33},{33,65},{65,97},{97,1},{2,34}... | collective-permute-start | bytes 1428488 | tf_op jit(solution)/shard_map/ppermute | solution.py:32
  48.6 52.1 %collective-permute-start.4 = (bf16[4,248,1920]{2,1,0:T(8,128)(2,1)S(1)}, bf16[4,248,1920]{2,1,0:T(8,128)(2,1)S(1)}, u32[]{:S(2)}, u32[]{:S(2)}) collective-permute-start(bf16[4,248,1920]{2,1,0:T(8,128)(2,1)S(1)} %pad_maximum_fusion), channel_id=1, source_target_pairs={{0,16},{16,0},{1,17},{17,1},{2,18},{18,2},{3,19},{19,3},{4,20},{20... | collective-permute-start | bytes 11427848 | tf_op jit(solution)/shard_map/ppermute | solution.py:38
  48.7 48.1 %collective-permute-start.5 = (bf16[1,248,1920]{2,1,0:T(8,128)(2,1)S(1)}, bf16[1,248,1920]{2,1,0:T(8,128)(2,1)}, u32[]{:S(2)}, u32[]{:S(2)}) collective-permute-start(bf16[1,248,1920]{2,1,0:T(8,128)(2,1)S(1)} %get-tuple-element.15), channel_id=1, source_target_pairs={{0,128},{128,0},{1,129},{129,1},{2,130},{130,2},{3,131},{131,3},{4... | collective-permute-start | bytes 2856968 | tf_op jit(solution)/shard_map/ppermute | solution.py:48
  96.8 20.0 %collective-permute-start.7 = (bf16[1,248,1920]{2,1,0:T(8,128)(2,1)}, bf16[1,248,1920]{2,1,0:T(8,128)(2,1)S(1)}, u32[]{:S(2)}, u32[]{:S(2)}) collective-permute-start(bf16[1,248,1920]{2,1,0:T(8,128)(2,1)} %collective-permute-done.5), channel_id=1, source_target_pairs={{0,96},{32,0},{64,32},{96,64},{1,97},{33,1},{65,33},{97,65},{2,98}... | collective-permute-start | bytes 2856968 | tf_op jit(solution)/shard_map/ppermute | solution.py:26
  99.8 19.2 %collective-permute-start.6 = (bf16[1,248,1920]{2,1,0:T(8,128)(2,1)}, bf16[1,248,1920]{2,1,0:T(8,128)(2,1)}, u32[]{:S(2)}, u32[]{:S(2)}) collective-permute-start(bf16[1,248,1920]{2,1,0:T(8,128)(2,1)} %collective-permute-done.5), channel_id=1, source_target_pairs={{0,32},{32,64},{64,96},{96,0},{1,33},{33,65},{65,97},{97,1},{2,34}... | collective-permute-start | bytes 2856968 | tf_op jit(solution)/shard_map/ppermute | solution.py:25
  120.3 9.3 %collective-permute-start.9 = (bf16[1,248,960]{2,1,0:T(8,128)(2,1)S(1)}, bf16[1,248,960]{2,1,0:T(8,128)(2,1)S(1)}, u32[]{:S(2)}, u32[]{:S(2)}) collective-permute-start(bf16[1,248,960]{2,1,0:T(8,128)(2,1)S(1)} %slice.29), channel_id=1, source_target_pairs={{0,96},{32,0},{64,32},{96,64},{1,97},{33,1},{65,33},{97,65},{2,98}... | collective-permute-start | bytes 1428488 | tf_op jit(solution)/shard_map/ppermute | solution.py:33
  122.2 9.0 %collective-permute-start.8 = (bf16[1,248,960]{2,1,0:T(8,128)(2,1)S(1)}, bf16[1,248,960]{2,1,0:T(8,128)(2,1)S(1)}, u32[]{:S(2)}, u32[]{:S(2)}) collective-permute-start(bf16[1,248,960]{2,1,0:T(8,128)(2,1)S(1)} %slice.28), channel_id=1, source_target_pairs={{0,32},{32,64},{64,96},{96,0},{1,33},{33,65},{65,97},{97,1},{2,34}... | collective-permute-start | bytes 1428488 | tf_op jit(solution)/shard_map/ppermute | solution.py:32
  134.3 6.7 %collective-permute-start.10 = (bf16[4,248,1920]{2,1,0:T(8,128)(2,1)S(1)}, bf16[4,248,1920]{2,1,0:T(8,128)(2,1)S(1)}, u32[]{:S(2)}, u32[]{:S(2)}) collective-permute-start(bf16[4,248,1920]{2,1,0:T(8,128)(2,1)S(1)} %pad_maximum_fusion.1), channel_id=1, source_target_pairs={{0,16},{16,0},{1,17},{17,1},{2,18},{18,2},{3,19},{19,3},{4,20},{20... | collective-permute-start | bytes 11427848 | tf_op jit(solution)/shard_map/ppermute | solution.py:38

commit v8 on v7

--- a/solution.py
+++ b/solution.py
@@ -36,7 +36,7 @@
     )
     chip = jnp.concatenate([blocks, from_below, far, from_above], axis=0)
     other_core = lax.ppermute(chip, "core", [(0, 1), (1, 0)])
-    return jnp.concatenate([chip, other_core], axis=0), after
+    return (chip, other_core), after
 
 
 def ladder(row_codes, row_scales, panel_codes, panel_scales, amplitudes):
@@ -48,14 +48,15 @@
     other = lax.ppermute(mine, "z_hi", [(i, (i + 1) % halves) for i in range(halves)])
     total = None
     for blocks in (mine, other):
-        gathered, total = gather_y_core(blocks, total)
-        half = jnp.einsum(
-            "qac,pdc->pqda", gathered[:, :rows], amplitudes, preferred_element_type=jnp.float32
-        ).astype(jnp.bfloat16)
-        part = jnp.einsum(
-            "qdb,pqda->bpa", gathered[:, rows:], half, preferred_element_type=jnp.float32
-        )
-        total = part if total is None else total + part
+        pieces, total = gather_y_core(blocks, total)
+        for gathered in pieces:
+            half = jnp.einsum(
+                "qac,pdc->pqda", gathered[:, :rows], amplitudes, preferred_element_type=jnp.float32
+            ).astype(jnp.bfloat16)
+            part = jnp.einsum(
+                "qdb,pqda->bpa", gathered[:, rows:], half, preferred_element_type=jnp.float32
+            )
+            total = part if total is None else total + part
     across, along = lax.axis_size("x"), lax.axis_size("z_lo")
     width = total.shape[0] // (across * along)
     sent = total.astype(jnp.bfloat16).reshape(across, along, width, *total.shape[1:])

time: 213 us -> 210 us (0.986)
  local copies, waits for them, and re-layouts: 20 us -> 8.13 us
  matrix products: 19 us -> 26.7 us
  other arithmetic: 13.3 us -> 15.7 us
    unnamed x10 -> x7, local copies, waits for them, and re-layouts: 8.41 us -> 0.84 us
    ppermute x2, waiting for transfers between devices: 11.7 us -> 17.3 us  [gather_y_core(): lax.ppermute(from_above[:, :, cut:], 'y', down)]
    ppermute x2, waiting for transfers between devices: 5.6 us -> 0.59 us  [gather_y_core(): other_core = lax.ppermute(chip, 'core', [(0, 1), (1, 0)])]
    dot_general x2 -> x4, matrix products: 19 us -> 23.8 us  [ladder(): jnp.einsum('qdb,pqda->bpa', gathered[:, rows:], half, preferred_element_t...]
    concatenate x2, other arithmetic: 2.65 us -> 7.26 us  [gather_y_core(): chip = jnp.concatenate([blocks, from_below, far, from_above], axis=0)]
    concatenate x2 -> x0, local copies, waits for them, and re-layouts: 4.27 us -> none  [gather_y_core(): return (jnp.concatenate([chip, other_core], axis=0), after)]
    dot_general x0 -> x1, matrix products: none -> 2.91 us  [ladder(): jnp.einsum('qac,pdc->pqda', gathered[:, :rows], amplitudes, preferred_ele...]
    unnamed x2 -> x0, other arithmetic: 2.48 us -> none
  transfers between devices with their start and end apart: 11 -> 11, of which waited for: 10 -> 10; matrix products, arithmetic and copies ran while one was open for 9% -> 10% of each run, Pallas kernels for 0% -> 0%
where the time goes in v8:
time: 210 us; the launch traced here: 209 us
  waiting for transfers between devices  89.4 us (43%)
  blocking collectives  52.2 us (25%)
  matrix products  26.7 us (13%)
  starting transfers between devices  16.7 us (8%)
  other arithmetic  15.7 us (7%)
  local copies, waits for them, and re-layouts  8.13 us (4%)
    ppermute x1, waiting for transfers between devices, ladder(): lax.ppermute(mine, 'z_hi', [(i, (i + 1) % halves) for i in range(halves)])  40.9 us
    all_to_all x1, blocking collectives, ladder(): got = lax.all_to_all(sent, 'x', 0, 0, tiled=True)  29.4 us
    ppermute x2, waiting for transfers between devices, gather_y_core(): from_above = lax.ppermute(blocks, 'y', down)  23.8 us
    dot_general x4, matrix products, ladder(): jnp.einsum('qdb,pqda->bpa', gathered[:, rows:], half, preferred_element_t...  23.8 us
    all_to_all x1, blocking collectives, ladder(): got = lax.all_to_all(summed, 'z_lo', 0, 0, tiled=True)  22.8 us
    ppermute x2, waiting for transfers between devices, gather_y_core(): lax.ppermute(from_above[:, :, cut:], 'y', down)  17.3 us
    concatenate x2, other arithmetic, gather_y_core(): chip = jnp.concatenate([blocks, from_below, far, from_above], axis=0)  7.26 us
    ppermute x1, starting transfers between devices, ladder(): lax.ppermute(mine, 'z_hi', [(i, (i + 1) % halves) for i in range(halves)])  7.19 us
  transfers between devices with their start and end apart: 11, of which 10 were waited for; matrix products, arithmetic and copies ran while one was open for 10% of the time, Pallas kernels for 0%

profile of v8, /device:TPU:8, one launch (start us, length us, event | category | flops | bytes accessed | tf_op | source)
XLA Modules:
  0.0 209.0 jit_solution(11399576936410885157)
XLA Ops:
  0.0 0.0 copy-start
  0.0 0.8 copy.31
  0.8 0.8 copy.26
  1.6 0.0 copy-start.2
  1.6 0.3 mul.37
  2.0 1.1 mul.38
  3.1 1.0 mul.33
  4.1 1.5 copy.14
  5.6 1.4 multiply_convert_fusion.1
  7.0 0.0 copy-done.2
  7.0 0.1 multiply_convert_fusion
  7.1 0.1 pad_maximum_fusion.2
  7.2 2.2 %collective-permute-start.2 = (bf16[1,248,1920]{2,1,0:T(8,128)(2,1)S(1)}, bf16[1,248,1920]{2,1,0:T(8,128)(2,1)S(1)}, u32[]{:S(2)}, u32[]{:S(2)}) collective-permute-start(bf16[1,248,1920]{2,1,0:T(8,128)(2,1)S(1)} %pad_maximum_fusion.2), channel_id=1, source_target_pairs={{0,96},{32,0},{64,32},{96,64},{1,97},{33,1},{65,33},{97,65},{2,98}... | collective-permute-start | bytes 2856968 | tf_op jit(solution)/shard_map/ppermute | solution.py:26
  9.4 0.0 collective-permute-start
  9.4 20.7 %collective-permute-done.2 = bf16[1,248,1920]{2,1,0:T(8,128)(2,1)S(1)} collective-permute-done((bf16[1,248,1920]{2,1,0:T(8,128)(2,1)S(1)}, bf16[1,248,1920]{2,1,0:T(8,128)(2,1)S(1)}, u32[]{:S(2)}, u32[]{:S(2)}) %collective-permute-start.2) | collective-permute-done | bytes 952352 | tf_op jit(solution)/shard_map/ppermute | solution.py:26
  30.1 0.2 slice.49
  30.3 1.1 collective-permute-start.3
  31.4 0.2 collective-permute-done
  31.5 0.1 slice.48
  31.6 1.0 collective-permute-start.1
  32.6 10.3 %collective-permute-done.3 = bf16[1,248,960]{2,1,0:T(8,128)(2,1)S(1)} collective-permute-done((bf16[1,248,960]{2,1,0:T(8,128)(2,1)S(1)}, bf16[1,248,960]{2,1,0:T(8,128)(2,1)S(1)}, u32[]{:S(2)}, u32[]{:S(2)}) %collective-permute-start.3) | collective-permute-done | bytes 476192 | tf_op jit(solution)/shard_map/ppermute | solution.py:33
  42.8 2.8 %collective-permute-done.1 = bf16[1,248,960]{2,1,0:T(8,128)(2,1)S(1)} collective-permute-done((bf16[1,248,960]{2,1,0:T(8,128)(2,1)S(1)}, bf16[1,248,960]{2,1,0:T(8,128)(2,1)S(1)}, u32[]{:S(2)}, u32[]{:S(2)}) %collective-permute-start.1) | collective-permute-done | bytes 476192 | tf_op jit(solution)/shard_map/ppermute | solution.py:32
  45.6 3.2 %fusion.4 = bf16[4,248,1920]{2,1,0:T(8,128)(2,1)} fusion(bf16[1,248,960]{2,1,0:T(8,128)(2,1)S(1)} %collective-permute-done.3, bf16[1,248,960]{2,1,0:T(8,128)(2,1)S(1)} %collective-permute-done.1, bf16[1,248,1920]{2,1,0:T(8,128)(2,1)S(1)} %collective-permute-done.2, bf16[1,248,1920]{2,1,0:T(8,128)(2,1)S(1)} %collective-permute-done, ...), kind=kLoop, calls=%fused_computation.9 | loop fusion | flops 22855680 | bytes 7618560 | tf_op jit(solution)/shard_map/concatenate | solution.py:37
  48.9 0.0 collective-permute-start.4
  48.9 7.2 %collective-permute-start.5 = (bf16[1,248,1920]{2,1,0:T(8,128)(2,1)S(1)}, bf16[1,248,1920]{2,1,0:T(8,128)(2,1)}, u32[]{:S(2)}, u32[]{:S(2)}) collective-permute-start(bf16[1,248,1920]{2,1,0:T(8,128)(2,1)S(1)} %pad_maximum_fusion.2), channel_id=1, source_target_pairs={{0,128},{128,0},{1,129},{129,1},{2,130},{130,2},{3,131},{131,3},{4... | collective-permute-start | bytes 2856968 | tf_op jit(solution)/shard_map/ppermute | solution.py:48
  56.1 40.9 %collective-permute-done.5 = bf16[1,248,1920]{2,1,0:T(8,128)(2,1)} collective-permute-done((bf16[1,248,1920]{2,1,0:T(8,128)(2,1)S(1)}, bf16[1,248,1920]{2,1,0:T(8,128)(2,1)}, u32[]{:S(2)}, u32[]{:S(2)}) %collective-permute-start.5) | collective-permute-done | bytes 952352 | tf_op jit(solution)/shard_map/ppermute | solution.py:48
  97.0 3.0 %collective-permute-start.7 = (bf16[1,248,1920]{2,1,0:T(8,128)(2,1)}, bf16[1,248,1920]{2,1,0:T(8,128)(2,1)S(1)}, u32[]{:S(2)}, u32[]{:S(2)}) collective-permute-start(bf16[1,248,1920]{2,1,0:T(8,128)(2,1)} %collective-permute-done.5), channel_id=1, source_target_pairs={{0,96},{32,0},{64,32},{96,64},{1,97},{33,1},{65,33},{97,65},{2,98}... | collective-permute-start | bytes 2856968 | tf_op jit(solution)/shard_map/ppermute | solution.py:26
  99.9 0.0 collective-permute-start.6
  99.9 0.0 copy-done
  99.9 6.4 %fusion.11 = f32[1920,4,128,1]{2,0,3,1:T(8,128)} fusion(bf16[4,248,1920]{2,1,0:T(8,128)(2,1)} %fusion.4, bf16[4,120,1920]{2,1,0:T(8,128)(2,1)S(1)} %copy-done), kind=kOutput, calls=%fused_computation.24 | convolution fusion | flops 1887682560 | bytes 9584640 | tf_op jit(solution)/shard_map/qdb,pqda->bpa/dot_general | solution.py:56
  106.3 0.0 copy-start.1
  106.3 0.0 collective-permute-done.4
  106.3 2.9 %fusion.34 = bf16[4,4,120,128]{3,2,1,0:T(8,128)(2,1)S(1)} fusion(bf16[4,120,1920]{2,1,0:T(8,128)(2,1)S(1)} %copy-done, bf16[4,248,1920]{2,1,0:T(8,128)(2,1)} %collective-permute-done.4), kind=kOutput, calls=%fused_computation.35 | convolution fusion | flops 943964160 | bytes 4300800 | tf_op jit(solution)/shard_map/qac,pdc->pqda/dot_general | solution.py:53
  109.2 0.0 copy-done.1
  109.2 4.6 %bitcast_add_fusion.2 = f32[1920,4,128]{2,0,1:T(8,128)} fusion(f32[1920,4,128,1]{2,0,3,1:T(8,128)S(1)} %copy-done.1, bf16[4,4,120,128]{3,2,1,0:T(8,128)(2,1)S(1)} %fusion.34, bf16[4,248,1920]{2,1,0:T(8,128)(2,1)} %collective-permute-done.4), kind=kOutput, calls=%fused_computation.3 | convolution fusion | flops 944701440 | bytes 10199040 | tf_op jit(solution)/shard_map/qdb,pqda->bpa/dot_general | solution.py:56
  113.8 3.1 %collective-permute-done.7 = bf16[1,248,1920]{2,1,0:T(8,128)(2,1)S(1)} collective-permute-done((bf16[1,248,1920]{2,1,0:T(8,128)(2,1)}, bf16[1,248,1920]{2,1,0:T(8,128)(2,1)S(1)}, u32[]{:S(2)}, u32[]{:S(2)}) %collective-permute-start.7) | collective-permute-done | bytes 952352 | tf_op jit(solution)/shard_map/ppermute | solution.py:26
  117.0 2.5 %collective-permute-done.6 = bf16[1,248,1920]{2,1,0:T(8,128)(2,1)} collective-permute-done((bf16[1,248,1920]{2,1,0:T(8,128)(2,1)}, bf16[1,248,1920]{2,1,0:T(8,128)(2,1)}, u32[]{:S(2)}, u32[]{:S(2)}) %collective-permute-start.6) | collective-permute-done | bytes 952352 | tf_op jit(solution)/shard_map/ppermute | solution.py:25
  119.5 1.1 slice.42
  120.5 0.2 slice.43
  120.7 1.6 collective-permute-start.9
  122.4 0.7 collective-permute-start.8
  123.0 7.0 %collective-permute-done.9 = bf16[1,248,960]{2,1,0:T(8,128)(2,1)S(1)} collective-permute-done((bf16[1,248,960]{2,1,0:T(8,128)(2,1)S(1)}, bf16[1,248,960]{2,1,0:T(8,128)(2,1)S(1)}, u32[]{:S(2)}, u32[]{:S(2)}) %collective-permute-start.9) | collective-permute-done | bytes 476192 | tf_op jit(solution)/shard_map/ppermute | solution.py:33
  130.0 1.4 collective-permute-done.8
  131.4 4.0 %fusion.2 = bf16[4,248,1920]{2,1,0:T(8,128)(2,1)} fusion(bf16[1,248,960]{2,1,0:T(8,128)(2,1)S(1)} %collective-permute-done.9, bf16[1,248,960]{2,1,0:T(8,128)(2,1)S(1)} %collective-permute-done.8, bf16[1,248,1920]{2,1,0:T(8,128)(2,1)S(1)} %collective-permute-done.7, bf16[1,248,1920]{2,1,0:T(8,128)(2,1)} %collective-permute-done.6, ...), kind=kLoop, calls=%fused_computation.6 | loop fusion | flops 19046400 | bytes 7618560 | tf_op jit(solution)/shard_map/concatenate | solution.py:37
  135.4 0.0 collective-permute-start.10
  135.4 6.4 %fusion.10 = f32[1920,4,128,1]{2,0,3,1:T(8,128)} fusion(bf16[4,248,1920]{2,1,0:T(8,128)(2,1)} %fusion.2, bf16[4,120,1920]{2,1,0:T(8,128)(2,1)S(1)} %copy-done), kind=kOutput, calls=%fused_computation.21 | convolution fusion | flops 1887682560 | bytes 9584640 | tf_op jit(solution)/shard_map/qdb,pqda->bpa/dot_general | solution.py:56
  141.8 0.6 collective-permute-done.10
  142.3 6.5 %fusion.9 = f32[1920,4,128,1]{2,0,3,1:T(8,128)} fusion(bf16[4,248,1920]{2,1,0:T(8,128)(2,1)} %collective-permute-done.10, bf16[4,120,1920]{2,1,0:T(8,128)(2,1)S(1)} %copy-done), kind=kOutput, calls=%fused_computation.19 | convolution fusion | flops 1887682560 | bytes 9584640 | tf_op jit(solution)/shard_map/qdb,pqda->bpa/dot_general | solution.py:56
  148.8 5.0 %fusion = bf16[1920,4,128]{2,0,1:T(8,128)(2,1)S(1)} fusion(f32[1920,4,128,1]{2,0,3,1:T(8,128)} %fusion.9, f32[1920,4,128]{2,0,1:T(8,128)} %bitcast_add_fusion.2, f32[1920,4,128,1]{2,0,3,1:T(8,128)} %fusion.10), kind=kLoop, calls=%fused_computation.1 | loop fusion | flops 2949120 | bytes 13762560 | tf_op jit(solution)/shard_map/convert_element_type | solution.py:62
  153.8 0.2 copy.16
  154.0 29.4 %all_to_all.10 = bf16[4,4,120,4,128]{4,2,1,3,0:T(8,128)(2,1)} all-to-all(bf16[4,4,120,4,128]{4,2,1,3,0:T(8,128)(2,1)S(1)} %copy.16), channel_id=1, replica_groups=mesh['z_hi'=2,'y'=4,'core'=2,'x'=4,'z_lo'=4] {'x'}, dimensions={0} | all-to-all | bytes 3932160 | tf_op jit(solution)/shard_map/all_to_all | solution.py:63
  183.4 1.9 reduce_sum.21
  185.3 22.8 %all_to_all.11 = bf16[4,120,4,128]{3,1,2,0:T(8,128)(2,1)S(1)} all-to-all(bf16[4,120,4,128]{3,1,2,0:T(8,128)(2,1)S(1)} %copy.18), channel_id=1, replica_groups=mesh['z_hi'=2,'y'=4,'core'=2,'x'=4,'z_lo'=4] {'z_lo'}, dimensions={0} | all-to-all | bytes 983040 | tf_op jit(solution)/shard_map/all_to_all | solution.py:65
  208.1 0.1 convert_reduce_fusion
  208.2 0.8 copy.20
  (1 shorter events, 0.0 us)
Async XLA Ops:
  0.0 99.9 %copy-start = (bf16[4,120,1920]{2,1,0:T(8,128)(2,1)S(1)}, bf16[4,120,1920]{2,1,0:T(8,128)(2,1)}, u32[]{:S(2)}) copy-start(bf16[4,120,1920]{2,1,0:T(8,128)(2,1)} %param.9) | copy-start | bytes 5529604
  1.6 5.4 %copy-start.2 = (bf16[1,128,1920]{2,1,0:T(8,128)(2,1)S(1)}, bf16[1,128,1920]{2,1,0:T(8,128)(2,1)}, u32[]{:S(2)}) copy-start(bf16[1,128,1920]{2,1,0:T(8,128)(2,1)} %param.5) | copy-start | bytes 1474564
  7.2 22.9 %collective-permute-start.2 = (bf16[1,248,1920]{2,1,0:T(8,128)(2,1)S(1)}, bf16[1,248,1920]{2,1,0:T(8,128)(2,1)S(1)}, u32[]{:S(2)}, u32[]{:S(2)}) collective-permute-start(bf16[1,248,1920]{2,1,0:T(8,128)(2,1)S(1)} %pad_maximum_fusion.2), channel_id=1, source_target_pairs={{0,96},{32,0},{64,32},{96,64},{1,97},{33,1},{65,33},{97,65},{2,98}... | collective-permute-start | bytes 2856968 | tf_op jit(solution)/shard_map/ppermute | solution.py:26
  9.4 22.1 %collective-permute-start = (bf16[1,248,1920]{2,1,0:T(8,128)(2,1)S(1)}, bf16[1,248,1920]{2,1,0:T(8,128)(2,1)S(1)}, u32[]{:S(2)}, u32[]{:S(2)}) collective-permute-start(bf16[1,248,1920]{2,1,0:T(8,128)(2,1)S(1)} %pad_maximum_fusion.2), channel_id=1, source_target_pairs={{0,32},{32,64},{64,96},{96,0},{1,33},{33,65},{65,97},{97,1},{2,34}... | collective-permute-start | bytes 2856968 | tf_op jit(solution)/shard_map/ppermute | solution.py:25
  30.3 12.5 %collective-permute-start.3 = (bf16[1,248,960]{2,1,0:T(8,128)(2,1)S(1)}, bf16[1,248,960]{2,1,0:T(8,128)(2,1)S(1)}, u32[]{:S(2)}, u32[]{:S(2)}) collective-permute-start(bf16[1,248,960]{2,1,0:T(8,128)(2,1)S(1)} %slice.49), channel_id=1, source_target_pairs={{0,96},{32,0},{64,32},{96,64},{1,97},{33,1},{65,33},{97,65},{2,98}... | collective-permute-start | bytes 1428488 | tf_op jit(solution)/shard_map/ppermute | solution.py:33
  31.6 14.0 %collective-permute-start.1 = (bf16[1,248,960]{2,1,0:T(8,128)(2,1)S(1)}, bf16[1,248,960]{2,1,0:T(8,128)(2,1)S(1)}, u32[]{:S(2)}, u32[]{:S(2)}) collective-permute-start(bf16[1,248,960]{2,1,0:T(8,128)(2,1)S(1)} %slice.48), channel_id=1, source_target_pairs={{0,32},{32,64},{64,96},{96,0},{1,33},{33,65},{65,97},{97,1},{2,34}... | collective-permute-start | bytes 1428488 | tf_op jit(solution)/shard_map/ppermute | solution.py:32
  48.9 57.4 %collective-permute-start.4 = (bf16[4,248,1920]{2,1,0:T(8,128)(2,1)}, bf16[4,248,1920]{2,1,0:T(8,128)(2,1)}, u32[]{:S(2)}, u32[]{:S(2)}) collective-permute-start(bf16[4,248,1920]{2,1,0:T(8,128)(2,1)} %fusion.4), channel_id=1, source_target_pairs={{0,16},{16,0},{1,17},{17,1},{2,18},{18,2},{3,19},{19,3},{4,20},{20... | collective-permute-start | bytes 11427848 | tf_op jit(solution)/shard_map/ppermute | solution.py:38
  48.9 48.1 %collective-permute-start.5 = (bf16[1,248,1920]{2,1,0:T(8,128)(2,1)S(1)}, bf16[1,248,1920]{2,1,0:T(8,128)(2,1)}, u32[]{:S(2)}, u32[]{:S(2)}) collective-permute-start(bf16[1,248,1920]{2,1,0:T(8,128)(2,1)S(1)} %pad_maximum_fusion.2), channel_id=1, source_target_pairs={{0,128},{128,0},{1,129},{129,1},{2,130},{130,2},{3,131},{131,3},{4... | collective-permute-start | bytes 2856968 | tf_op jit(solution)/shard_map/ppermute | solution.py:48
  97.0 20.0 %collective-permute-start.7 = (bf16[1,248,1920]{2,1,0:T(8,128)(2,1)}, bf16[1,248,1920]{2,1,0:T(8,128)(2,1)S(1)}, u32[]{:S(2)}, u32[]{:S(2)}) collective-permute-start(bf16[1,248,1920]{2,1,0:T(8,128)(2,1)} %collective-permute-done.5), channel_id=1, source_target_pairs={{0,96},{32,0},{64,32},{96,64},{1,97},{33,1},{65,33},{97,65},{2,98}... | collective-permute-start | bytes 2856968 | tf_op jit(solution)/shard_map/ppermute | solution.py:26
  99.9 19.5 %collective-permute-start.6 = (bf16[1,248,1920]{2,1,0:T(8,128)(2,1)}, bf16[1,248,1920]{2,1,0:T(8,128)(2,1)}, u32[]{:S(2)}, u32[]{:S(2)}) collective-permute-start(bf16[1,248,1920]{2,1,0:T(8,128)(2,1)} %collective-permute-done.5), channel_id=1, source_target_pairs={{0,32},{32,64},{64,96},{96,0},{1,33},{33,65},{65,97},{97,1},{2,34}... | collective-permute-start | bytes 2856968 | tf_op jit(solution)/shard_map/ppermute | solution.py:25
  106.3 2.9 %copy-start.1 = (f32[1920,4,128,1]{2,0,3,1:T(8,128)S(1)}, f32[1920,4,128,1]{2,0,3,1:T(8,128)}, u32[]{:S(2)}) copy-start(f32[1920,4,128,1]{2,0,3,1:T(8,128)} %fusion.11) | copy-start | bytes 11796484
  120.7 9.3 %collective-permute-start.9 = (bf16[1,248,960]{2,1,0:T(8,128)(2,1)S(1)}, bf16[1,248,960]{2,1,0:T(8,128)(2,1)S(1)}, u32[]{:S(2)}, u32[]{:S(2)}) collective-permute-start(bf16[1,248,960]{2,1,0:T(8,128)(2,1)S(1)} %slice.43), channel_id=1, source_target_pairs={{0,96},{32,0},{64,32},{96,64},{1,97},{33,1},{65,33},{97,65},{2,98}... | collective-permute-start | bytes 1428488 | tf_op jit(solution)/shard_map/ppermute | solution.py:33
  122.4 9.0 %collective-permute-start.8 = (bf16[1,248,960]{2,1,0:T(8,128)(2,1)S(1)}, bf16[1,248,960]{2,1,0:T(8,128)(2,1)S(1)}, u32[]{:S(2)}, u32[]{:S(2)}) collective-permute-start(bf16[1,248,960]{2,1,0:T(8,128)(2,1)S(1)} %slice.42), channel_id=1, source_target_pairs={{0,32},{32,64},{64,96},{96,0},{1,33},{33,65},{65,97},{97,1},{2,34}... | collective-permute-start | bytes 1428488 | tf_op jit(solution)/shard_map/ppermute | solution.py:32
  135.4 7.0 %collective-permute-start.10 = (bf16[4,248,1920]{2,1,0:T(8,128)(2,1)}, bf16[4,248,1920]{2,1,0:T(8,128)(2,1)}, u32[]{:S(2)}, u32[]{:S(2)}) collective-permute-start(bf16[4,248,1920]{2,1,0:T(8,128)(2,1)} %fusion.2), channel_id=1, source_target_pairs={{0,16},{16,0},{1,17},{17,1},{2,18},{18,2},{3,19},{19,3},{4,20},{20... | collective-permute-start | bytes 11427848 | tf_op jit(solution)/shard_map/ppermute | solution.py:38

commit v9 on v8

--- a/solution.py
+++ b/solution.py
@@ -49,14 +49,19 @@
     total = None
     for blocks in (mine, other):
         pieces, total = gather_y_core(blocks, total)
-        for gathered in pieces:
-            half = jnp.einsum(
+        halves_of = [
+            jnp.einsum(
                 "qac,pdc->pqda", gathered[:, :rows], amplitudes, preferred_element_type=jnp.float32
             ).astype(jnp.bfloat16)
-            part = jnp.einsum(
-                "qdb,pqda->bpa", gathered[:, rows:], half, preferred_element_type=jnp.float32
-            )
-            total = part if total is None else total + part
+            for gathered in pieces
+        ]
+        part = jnp.einsum(
+            "qdb,pqda->bpa",
+            jnp.concatenate([gathered[:, rows:] for gathered in pieces], axis=0),
+            jnp.concatenate(halves_of, axis=1),
+            preferred_element_type=jnp.float32,
+        )
+        total = part if total is None else total + part
     across, along = lax.axis_size("x"), lax.axis_size("z_lo")
     width = total.shape[0] // (across * along)
     sent = total.astype(jnp.bfloat16).reshape(across, along, width, *total.shape[1:])

time: 210 us -> 197 us (0.938)
  matrix products: 26.7 us -> 9.39 us
  waiting for transfers between devices: 89.4 us -> 100 us
  other arithmetic: 15.7 us -> 7.44 us
    ppermute x2, waiting for transfers between devices: 2.64 us -> 32.1 us  [gather_y_core(): from_below = lax.ppermute(blocks, 'y', up)]
    ppermute x2, waiting for transfers between devices: 23.8 us -> 1.76 us  [gather_y_core(): from_above = lax.ppermute(blocks, 'y', down)]
    dot_general x4 -> x2, matrix products: 23.8 us -> 4.55 us  [ladder(): jnp.einsum('qdb,pqda->bpa', jnp.concatenate([gathered[:, rows:] for gathe...]
    ppermute x2, waiting for transfers between devices: 17.3 us -> 3.52 us  [gather_y_core(): lax.ppermute(from_above[:, :, cut:], 'y', down)]
    ppermute x2, waiting for transfers between devices: 4.15 us -> 16.7 us  [gather_y_core(): lax.ppermute(from_below[:, :, :cut], 'y', up)]
    ppermute x2, waiting for transfers between devices: 0.59 us -> 5.24 us  [gather_y_core(): other_core = lax.ppermute(chip, 'core', [(0, 1), (1, 0)])]
    convert_element_type x1, other arithmetic: 4.98 us -> 0.38 us  [ladder(): total.astype(jnp.bfloat16).reshape(across, along, width, *total.shape[1:])]
    ppermute x2, starting transfers between devices: 5.18 us -> 1.41 us  [gather_y_core(): from_above = lax.ppermute(blocks, 'y', down)]
  transfers between devices with their start and end apart: 11 -> 11, of which waited for: 10 -> 9; matrix products, arithmetic and copies ran while one was open for 10% -> 3% of each run, Pallas kernels for 0% -> 0%
where the time goes in v9:
time: 197 us; the launch traced here: 196 us
  waiting for transfers between devices  100 us (51%)
  blocking collectives  53.1 us (27%)
  starting transfers between devices  16.4 us (8%)
  local copies, waits for them, and re-layouts  9.82 us (5%)
  matrix products  9.39 us (5%)
  other arithmetic  7.44 us (4%)
    ppermute x1, waiting for transfers between devices, ladder(): lax.ppermute(mine, 'z_hi', [(i, (i + 1) % halves) for i in range(halves)])  40.8 us
    ppermute x2, waiting for transfers between devices, gather_y_core(): from_below = lax.ppermute(blocks, 'y', up)  32.1 us
    all_to_all x1, blocking collectives, ladder(): got = lax.all_to_all(sent, 'x', 0, 0, tiled=True)  29.4 us
    all_to_all x1, blocking collectives, ladder(): got = lax.all_to_all(summed, 'z_lo', 0, 0, tiled=True)  23.7 us
    ppermute x2, waiting for transfers between devices, gather_y_core(): lax.ppermute(from_below[:, :, :cut], 'y', up)  16.7 us
    ppermute x1, starting transfers between devices, ladder(): lax.ppermute(mine, 'z_hi', [(i, (i + 1) % halves) for i in range(halves)])  7.28 us
    mul x5, local copies, waits for them, and re-layouts, decode_rows(): codes.astype(jnp.float32).reshape(count, width, blocks, length // blocks)  6.93 us
    ppermute x2, waiting for transfers between devices, gather_y_core(): other_core = lax.ppermute(chip, 'core', [(0, 1), (1, 0)])  5.24 us
  transfers between devices with their start and end apart: 11, of which 9 were waited for; matrix products, arithmetic and copies ran while one was open for 3% of the time, Pallas kernels for 0%

profile of v9, /device:TPU:8, one launch (start us, length us, event | category | flops | bytes accessed | tf_op | source)
XLA Modules:
  0.0 196.5 jit_solution(1732832521695296677)
XLA Ops:
  0.0 0.0 copy-start
  0.0 0.0 copy-start.1
  0.0 0.8 copy.29
  0.9 1.0 mul.33
  1.9 1.5 copy.14
  3.4 0.8 copy.24
  4.2 1.3 mul.37
  5.5 2.3 %mul.38 = f32[1,120,1920]{2,1,0:T(8,128)} reshape(f32[120,15,128]{2,1,0:T(8,128)} %mul.37) | data formatting | bytes 1843200 | tf_op jit(solution)/shard_map/mul | solution.py:15
  7.8 0.0 copy-done.1
  7.8 0.1 multiply_convert_fusion
  7.9 1.4 multiply_convert_fusion.1
  9.3 0.1 pad_maximum_fusion.2
  9.3 1.7 collective-permute-start
  11.0 0.7 collective-permute-start.2
  11.7 20.6 %collective-permute-done = bf16[1,248,1920]{2,1,0:T(8,128)(2,1)S(1)} collective-permute-done((bf16[1,248,1920]{2,1,0:T(8,128)(2,1)S(1)}, bf16[1,248,1920]{2,1,0:T(8,128)(2,1)S(1)}, u32[]{:S(2)}, u32[]{:S(2)}) %collective-permute-start) | collective-permute-done | bytes 952352 | tf_op jit(solution)/shard_map/ppermute | solution.py:25
  32.2 0.1 slice.48
  32.3 1.7 collective-permute-start.1
  34.0 0.0 collective-permute-done.2
  34.0 0.2 slice.49
  34.2 0.5 collective-permute-start.3
  34.7 10.0 %collective-permute-done.1 = bf16[1,248,960]{2,1,0:T(8,128)(2,1)S(1)} collective-permute-done((bf16[1,248,960]{2,1,0:T(8,128)(2,1)S(1)}, bf16[1,248,960]{2,1,0:T(8,128)(2,1)S(1)}, u32[]{:S(2)}, u32[]{:S(2)}) %collective-permute-start.1) | collective-permute-done | bytes 476192 | tf_op jit(solution)/shard_map/ppermute | solution.py:32
  44.7 1.7 collective-permute-done.3
  46.4 2.0 %fusion.4 = bf16[4,248,1920]{2,1,0:T(8,128)(2,1)S(1)} fusion(bf16[1,248,960]{2,1,0:T(8,128)(2,1)S(1)} %collective-permute-done.3, bf16[1,248,960]{2,1,0:T(8,128)(2,1)S(1)} %collective-permute-done.1, bf16[1,248,1920]{2,1,0:T(8,128)(2,1)S(1)} %collective-permute-done.2, bf16[1,248,1920]{2,1,0:T(8,128)(2,1)S(1)} %collective-permute-done, ...), kind=kLoop, calls=%fused_computation.7 | loop fusion | flops 22855680 | bytes 7618560 | tf_op jit(solution)/shard_map/concatenate | solution.py:37
  48.5 0.1 collective-permute-start.4
  48.6 7.3 %collective-permute-start.5 = (bf16[1,248,1920]{2,1,0:T(8,128)(2,1)S(1)}, bf16[1,248,1920]{2,1,0:T(8,128)(2,1)S(1)}, u32[]{:S(2)}, u32[]{:S(2)}) collective-permute-start(bf16[1,248,1920]{2,1,0:T(8,128)(2,1)S(1)} %pad_maximum_fusion.2), channel_id=1, source_target_pairs={{0,128},{128,0},{1,129},{129,1},{2,130},{130,2},{3,131},{131,3},{4... | collective-permute-start | bytes 2856968 | tf_op jit(solution)/shard_map/ppermute | solution.py:48
  55.8 40.8 %collective-permute-done.5 = bf16[1,248,1920]{2,1,0:T(8,128)(2,1)S(1)} collective-permute-done((bf16[1,248,1920]{2,1,0:T(8,128)(2,1)S(1)}, bf16[1,248,1920]{2,1,0:T(8,128)(2,1)S(1)}, u32[]{:S(2)}, u32[]{:S(2)}) %collective-permute-start.5) | collective-permute-done | bytes 952352 | tf_op jit(solution)/shard_map/ppermute | solution.py:48
  96.6 1.3 collective-permute-start.6
  97.9 0.7 collective-permute-start.7
  98.7 0.0 copy-done
  98.7 1.2 fusion.41
  99.9 0.1 slice.50
  100.0 0.0 collective-permute-done.4
  100.0 0.1 slice.51
  100.2 1.2 fusion.38
  101.4 2.3 %fusion.11 = f32[1920,4,128]{2,0,1:T(8,128)S(1)} fusion(bf16[4,120,1920]{2,1,0:T(8,128)(2,1)S(1)} %slice.51, bf16[4,120,1920]{2,1,0:T(8,128)(2,1)S(1)} %slice.50, bf16[4,4,120,128]{3,2,1,0:T(8,128)(2,1)S(1)} %fusion.38, bf16[4,4,120,128]{3,2,1,0:T(8,128)(2,1)S(1)} %fusion.41), kind=kOutput, calls=%fused_computation.16 | convolution fusion | flops 1896775680 | bytes 8601600 | tf_op jit(solution)/shard_map/qdb,pqda->bpa/dot_general | solution.py:58
  103.7 11.5 %collective-permute-done.6 = bf16[1,248,1920]{2,1,0:T(8,128)(2,1)S(1)} collective-permute-done((bf16[1,248,1920]{2,1,0:T(8,128)(2,1)S(1)}, bf16[1,248,1920]{2,1,0:T(8,128)(2,1)S(1)}, u32[]{:S(2)}, u32[]{:S(2)}) %collective-permute-start.6) | collective-permute-done | bytes 952352 | tf_op jit(solution)/shard_map/ppermute | solution.py:25
  115.2 1.8 collective-permute-done.7
  117.0 0.1 slice.42
  117.0 1.8 collective-permute-start.8
  118.8 0.2 slice.43
  119.0 0.6 collective-permute-start.9
  119.6 6.7 %collective-permute-done.8 = bf16[1,248,960]{2,1,0:T(8,128)(2,1)S(1)} collective-permute-done((bf16[1,248,960]{2,1,0:T(8,128)(2,1)S(1)}, bf16[1,248,960]{2,1,0:T(8,128)(2,1)S(1)}, u32[]{:S(2)}, u32[]{:S(2)}) %collective-permute-start.8) | collective-permute-done | bytes 476192 | tf_op jit(solution)/shard_map/ppermute | solution.py:32
  126.3 1.8 collective-permute-done.9
  128.1 1.6 fusion.2
  129.7 0.1 collective-permute-start.10
  129.8 0.1 slice.54
  129.9 1.2 fusion.35
  131.1 5.2 %collective-permute-done.10 = bf16[4,248,1920]{2,1,0:T(8,128)(2,1)S(1)} collective-permute-done((bf16[4,248,1920]{2,1,0:T(8,128)(2,1)S(1)}, bf16[4,248,1920]{2,1,0:T(8,128)(2,1)S(1)}, u32[]{:S(2)}, u32[]{:S(2)}) %collective-permute-start.10) | collective-permute-done | bytes 3809312 | tf_op jit(solution)/shard_map/ppermute | solution.py:38
  136.3 0.1 slice.55
  136.5 1.2 fusion.32
  137.7 2.3 %fusion.8 = f32[1920,4,128,1]{2,0,3,1:T(8,128)S(1)} fusion(bf16[4,120,1920]{2,1,0:T(8,128)(2,1)S(1)} %slice.55, bf16[4,120,1920]{2,1,0:T(8,128)(2,1)S(1)} %slice.54, bf16[4,4,120,128]{3,2,1,0:T(8,128)(2,1)S(1)} %fusion.32, bf16[4,4,120,128]{3,2,1,0:T(8,128)(2,1)S(1)} %fusion.35), kind=kOutput, calls=%fused_computation.13 | convolution fusion | flops 1896775680 | bytes 8601600 | tf_op jit(solution)/shard_map/qdb,pqda->bpa/dot_general | solution.py:58
  140.0 0.4 fusion
  140.4 0.2 copy.16
  140.6 29.4 %all_to_all.10 = bf16[4,4,120,4,128]{4,2,1,3,0:T(8,128)(2,1)} all-to-all(bf16[4,4,120,4,128]{4,2,1,3,0:T(8,128)(2,1)S(1)} %copy.16), channel_id=1, replica_groups=mesh['z_hi'=2,'y'=4,'core'=2,'x'=4,'z_lo'=4] {'x'}, dimensions={0} | all-to-all | bytes 3932160 | tf_op jit(solution)/shard_map/all_to_all | solution.py:68
  170.0 1.9 reduce_sum.21
  171.9 23.7 %all_to_all.11 = bf16[4,120,4,128]{3,1,2,0:T(8,128)(2,1)S(1)} all-to-all(bf16[4,120,4,128]{3,1,2,0:T(8,128)(2,1)S(1)} %copy.18), channel_id=1, replica_groups=mesh['z_hi'=2,'y'=4,'core'=2,'x'=4,'z_lo'=4] {'z_lo'}, dimensions={0} | all-to-all | bytes 983040 | tf_op jit(solution)/shard_map/all_to_all | solution.py:70
  195.6 0.1 convert_reduce_fusion
  195.7 0.8 copy.20
  (1 shorter events, 0.0 us)
Async XLA Ops:
  0.0 98.7 %copy-start = (bf16[4,120,1920]{2,1,0:T(8,128)(2,1)S(1)}, bf16[4,120,1920]{2,1,0:T(8,128)(2,1)}, u32[]{:S(2)}) copy-start(bf16[4,120,1920]{2,1,0:T(8,128)(2,1)} %param.9) | copy-start | bytes 5529604
  0.0 7.8 %copy-start.1 = (bf16[1,128,1920]{2,1,0:T(8,128)(2,1)S(1)}, bf16[1,128,1920]{2,1,0:T(8,128)(2,1)}, u32[]{:S(2)}) copy-start(bf16[1,128,1920]{2,1,0:T(8,128)(2,1)} %param.5) | copy-start | bytes 1474564
  9.3 22.9 %collective-permute-start = (bf16[1,248,1920]{2,1,0:T(8,128)(2,1)S(1)}, bf16[1,248,1920]{2,1,0:T(8,128)(2,1)S(1)}, u32[]{:S(2)}, u32[]{:S(2)}) collective-permute-start(bf16[1,248,1920]{2,1,0:T(8,128)(2,1)S(1)} %pad_maximum_fusion.2), channel_id=1, source_target_pairs={{0,32},{32,64},{64,96},{96,0},{1,33},{33,65},{65,97},{97,1},{2,34}... | collective-permute-start | bytes 2856968 | tf_op jit(solution)/shard_map/ppermute | solution.py:25
  11.0 23.0 %collective-permute-start.2 = (bf16[1,248,1920]{2,1,0:T(8,128)(2,1)S(1)}, bf16[1,248,1920]{2,1,0:T(8,128)(2,1)S(1)}, u32[]{:S(2)}, u32[]{:S(2)}) collective-permute-start(bf16[1,248,1920]{2,1,0:T(8,128)(2,1)S(1)} %pad_maximum_fusion.2), channel_id=1, source_target_pairs={{0,96},{32,0},{64,32},{96,64},{1,97},{33,1},{65,33},{97,65},{2,98}... | collective-permute-start | bytes 2856968 | tf_op jit(solution)/shard_map/ppermute | solution.py:26
  32.3 12.4 %collective-permute-start.1 = (bf16[1,248,960]{2,1,0:T(8,128)(2,1)S(1)}, bf16[1,248,960]{2,1,0:T(8,128)(2,1)S(1)}, u32[]{:S(2)}, u32[]{:S(2)}) collective-permute-start(bf16[1,248,960]{2,1,0:T(8,128)(2,1)S(1)} %slice.48), channel_id=1, source_target_pairs={{0,32},{32,64},{64,96},{96,0},{1,33},{33,65},{65,97},{97,1},{2,34}... | collective-permute-start | bytes 1428488 | tf_op jit(solution)/shard_map/ppermute | solution.py:32
  34.2 12.3 %collective-permute-start.3 = (bf16[1,248,960]{2,1,0:T(8,128)(2,1)S(1)}, bf16[1,248,960]{2,1,0:T(8,128)(2,1)S(1)}, u32[]{:S(2)}, u32[]{:S(2)}) collective-permute-start(bf16[1,248,960]{2,1,0:T(8,128)(2,1)S(1)} %slice.49), channel_id=1, source_target_pairs={{0,96},{32,0},{64,32},{96,64},{1,97},{33,1},{65,33},{97,65},{2,98}... | collective-permute-start | bytes 1428488 | tf_op jit(solution)/shard_map/ppermute | solution.py:33
  48.5 51.6 %collective-permute-start.4 = (bf16[4,248,1920]{2,1,0:T(8,128)(2,1)S(1)}, bf16[4,248,1920]{2,1,0:T(8,128)(2,1)S(1)}, u32[]{:S(2)}, u32[]{:S(2)}) collective-permute-start(bf16[4,248,1920]{2,1,0:T(8,128)(2,1)S(1)} %fusion.4), channel_id=1, source_target_pairs={{0,16},{16,0},{1,17},{17,1},{2,18},{18,2},{3,19},{19,3},{4,20},{20... | collective-permute-start | bytes 11427848 | tf_op jit(solution)/shard_map/ppermute | solution.py:38
  48.6 48.1 %collective-permute-start.5 = (bf16[1,248,1920]{2,1,0:T(8,128)(2,1)S(1)}, bf16[1,248,1920]{2,1,0:T(8,128)(2,1)S(1)}, u32[]{:S(2)}, u32[]{:S(2)}) collective-permute-start(bf16[1,248,1920]{2,1,0:T(8,128)(2,1)S(1)} %pad_maximum_fusion.2), channel_id=1, source_target_pairs={{0,128},{128,0},{1,129},{129,1},{2,130},{130,2},{3,131},{131,3},{4... | collective-permute-start | bytes 2856968 | tf_op jit(solution)/shard_map/ppermute | solution.py:48
  96.6 18.6 %collective-permute-start.6 = (bf16[1,248,1920]{2,1,0:T(8,128)(2,1)S(1)}, bf16[1,248,1920]{2,1,0:T(8,128)(2,1)S(1)}, u32[]{:S(2)}, u32[]{:S(2)}) collective-permute-start(bf16[1,248,1920]{2,1,0:T(8,128)(2,1)S(1)} %collective-permute-done.5), channel_id=1, source_target_pairs={{0,32},{32,64},{64,96},{96,0},{1,33},{33,65},{65,97},{97,1},{2,34}... | collective-permute-start | bytes 2856968 | tf_op jit(solution)/shard_map/ppermute | solution.py:25
  97.9 19.0 %collective-permute-start.7 = (bf16[1,248,1920]{2,1,0:T(8,128)(2,1)S(1)}, bf16[1,248,1920]{2,1,0:T(8,128)(2,1)S(1)}, u32[]{:S(2)}, u32[]{:S(2)}) collective-permute-start(bf16[1,248,1920]{2,1,0:T(8,128)(2,1)S(1)} %collective-permute-done.5), channel_id=1, source_target_pairs={{0,96},{32,0},{64,32},{96,64},{1,97},{33,1},{65,33},{97,65},{2,98}... | collective-permute-start | bytes 2856968 | tf_op jit(solution)/shard_map/ppermute | solution.py:26
  117.0 9.3 %collective-permute-start.8 = (bf16[1,248,960]{2,1,0:T(8,128)(2,1)S(1)}, bf16[1,248,960]{2,1,0:T(8,128)(2,1)S(1)}, u32[]{:S(2)}, u32[]{:S(2)}) collective-permute-start(bf16[1,248,960]{2,1,0:T(8,128)(2,1)S(1)} %slice.42), channel_id=1, source_target_pairs={{0,32},{32,64},{64,96},{96,0},{1,33},{33,65},{65,97},{97,1},{2,34}... | collective-permute-start | bytes 1428488 | tf_op jit(solution)/shard_map/ppermute | solution.py:32
  119.0 9.1 %collective-permute-start.9 = (bf16[1,248,960]{2,1,0:T(8,128)(2,1)S(1)}, bf16[1,248,960]{2,1,0:T(8,128)(2,1)S(1)}, u32[]{:S(2)}, u32[]{:S(2)}) collective-permute-start(bf16[1,248,960]{2,1,0:T(8,128)(2,1)S(1)} %slice.43), channel_id=1, source_target_pairs={{0,96},{32,0},{64,32},{96,64},{1,97},{33,1},{65,33},{97,65},{2,98}... | collective-permute-start | bytes 1428488 | tf_op jit(solution)/shard_map/ppermute | solution.py:33
  129.7 6.7 %collective-permute-start.10 = (bf16[4,248,1920]{2,1,0:T(8,128)(2,1)S(1)}, bf16[4,248,1920]{2,1,0:T(8,128)(2,1)S(1)}, u32[]{:S(2)}, u32[]{:S(2)}) collective-permute-start(bf16[4,248,1920]{2,1,0:T(8,128)(2,1)S(1)} %fusion.2), channel_id=1, source_target_pairs={{0,16},{16,0},{1,17},{17,1},{2,18},{18,2},{3,19},{19,3},{4,20},{20... | collective-permute-start | bytes 11427848 | tf_op jit(solution)/shard_map/ppermute | solution.py:38
